TPU v7x, 256 devices: a whole 4x4x8 slice. The times are simulated.
256 devices in a mesh: replica: 8 (over y, core), fsdp: 32 (over x, z).
Axes of the slice: x: 4, y: 4, z: 8, core: 2. Of those that a mesh axis runs over, the one named last changes fastest.
Arguments:
- anchor_params: bfloat16 [24, 512, 4096], P(None, 'fsdp')
- replica_params: bfloat16 [8, 24, 512, 4096], P('replica', None, 'fsdp')
- projection: bfloat16 [4096, 384], replicated
- momentum: float32 [24, 512, 384], P(None, 'fsdp'), may hold values from -1.8 to 1.8
- rate_table: float32 [4, 6], replicated, may hold values from 0.1 to 1
- owner_list: int32 [24], replicated, may hold values from 0 to 31, as said below
- layer_kind: int32 [24, 2], replicated, may hold values from 0 to 5, as said below
Outputs:
- new_params: bfloat16 [24, 512, 4096], P(None, 'fsdp')
- new_momentum: float32 [24, 512, 384], P(None, 'fsdp')
Inputs may be any that keep to these rules, and one draw needn't show every extreme that they name: `owner_list`: no fsdp index is named more than 2 times, and in every draw some index is named exactly 2 times. `layer_kind`: column 0 is a layer, column 1 a kind below 6; each layer has 6 rows, and no two rows are equal.
All inputs are finite; a program needn't handle non-finite values.
Results may differ from a plain program's by a relative error of at most 0.0055.
Values may be sent and summed in bfloat16 or wider, within the bound.
No kernel may reach another device: no remote copies, remote signals or barrier semaphores. Data moves between devices by JAX's collectives and lax.ppermute only.
A program may use at most 128 MiB of HBM per device.

v0:
```python
import jax
import jax.numpy as jnp
from jax import lax
from jax.sharding import PartitionSpec as P

OUTER_MOMENTUM = 0.9
EPSILON = 1e-06


def decompress(direction, projection):
    flattened = direction.reshape(-1, direction.shape[-1])
    return lax.dot_general(
        flattened, projection, (((1,), (1,)), ((), ())), preferred_element_type=jnp.float32
    ).astype(jnp.bfloat16)


def local(anchor_params, replica_params, projection, momentum, rate_table, owner_list, layer_kind):
    matrices, rows_dev, model_width = anchor_params.shape
    rank_dim = projection.shape[1]
    fsdp_size = lax.axis_size("fsdp")
    own_bound = max(2, (matrices + fsdp_size - 1) // fsdp_size + 1)
    all_rows = rows_dev * fsdp_size
    highest = lax.Precision.HIGHEST
    pseudo_grad = (
        anchor_params.astype(jnp.float32) - replica_params[0].astype(jnp.float32)
    ).astype(jnp.bfloat16)
    compressed = jnp.dot(
        pseudo_grad.reshape(matrices * rows_dev, model_width),
        projection,
        preferred_element_type=jnp.float32,
    )
    summed = lax.psum(compressed.reshape(matrices, rows_dev, rank_dim), "replica")
    outer_grad = summed / lax.axis_size("replica")
    new_momentum = OUTER_MOMENTUM * momentum + outer_grad
    outer_step = outer_grad + OUTER_MOMENTUM * new_momentum
    same_group = (owner_list[:, None] == owner_list[None, :]).astype(jnp.float32)
    layer_onehot = (layer_kind[:, 0:1] == jnp.arange(rate_table.shape[0])[None, :]).astype(
        jnp.float32
    )
    kind_onehot = (layer_kind[:, 1:2] == jnp.arange(rate_table.shape[1])[None, :]).astype(
        jnp.float32
    )
    outer_rate = jnp.sum(jnp.dot(layer_onehot, rate_table, precision=highest) * kind_onehot, axis=1)
    own_index = lax.axis_index("fsdp")
    earlier = jnp.arange(matrices)[:, None] > jnp.arange(matrices)[None, :]
    position = jnp.sum(jnp.where(earlier, same_group, 0.0), axis=1).astype(jnp.int32)
    slot_of = owner_list * own_bound + position
    slot_ids = jnp.arange(fsdp_size * own_bound, dtype=jnp.int32)
    picker = (slot_ids[:, None] == slot_of[None, :]).astype(jnp.float32)
    outgoing = jnp.dot(picker, outer_step.reshape(matrices, -1), precision=highest).reshape(
        fsdp_size, own_bound, rows_dev, rank_dim
    )
    incoming = lax.all_to_all(outgoing, "fsdp", split_axis=0, concat_axis=0, tiled=True)
    own_slots = own_index * own_bound + jnp.arange(own_bound, dtype=jnp.int32)
    owned_slots = (slot_of[None, :] == own_slots[:, None]).astype(jnp.float32)
    owned_count = jnp.maximum(jnp.sum(owned_slots), 1.0)
    group_squares = jnp.sum(incoming * incoming)
    scaling = lax.rsqrt(group_squares / (owned_count * (all_rows * rank_dim)) + EPSILON)
    slot_rate = jnp.dot(owned_slots, outer_rate, precision=highest)
    slot_direction = (incoming * (slot_rate * scaling)[None, :, None, None]).astype(jnp.bfloat16)
    back_picker = picker.T.astype(jnp.bfloat16)
    slot_update = decompress(slot_direction, projection).reshape(
        fsdp_size, own_bound, rows_dev, model_width
    )
    returned = lax.all_to_all(slot_update, "fsdp", split_axis=0, concat_axis=0, tiled=True)
    update = (
        jnp.dot(
            back_picker,
            returned.reshape(fsdp_size * own_bound, -1),
            preferred_element_type=jnp.float32,
        )
        .astype(jnp.bfloat16)
        .reshape(matrices, rows_dev, model_width)
    )
    new_params = (anchor_params.astype(jnp.float32) - update.astype(jnp.float32)).astype(
        jnp.bfloat16
    )
    return (new_params, new_momentum)


def solution(mesh):
    placed = (
        P(None, "fsdp", None),
        P("replica", None, "fsdp", None),
        P(),
        P(None, "fsdp", None),
        P(),
        P(),
        P(),
    )
    return jax.shard_map(
        local,
        mesh=mesh,
        in_specs=placed,
        out_specs=(P(None, "fsdp", None), P(None, "fsdp", None)),
        check_vma=False,
    )
```

profile of v0, /device:TPU:24, one launch (start us, length us, event | category | flops | bytes accessed | tf_op | source)
XLA Modules:
  0.0 368.5 jit_solution(15477138471797277751)
XLA Ops:
  7.2 0.0 copy-start
  7.2 0.0 copy-start.4
  7.2 0.0 all-reduce.2.cloned.1.call-start
  7.2 1.8 copy-done
  9.1 5.4 %fusion.3 = f32[24,16,384]{2,1,0:T(8,128)} fusion(bf16[24,16,4096]{2,1,0:T(8,128)(2,1)} %param.7, bf16[1,24,16,4096]{3,2,1,0:T(8,128)(2,1)} %param.8, bf16[4096,384]{1,0:T(8,128)(2,1)S(1)} %copy-done), kind=kOutput, calls=%fused_computation.7 | convolution fusion | flops 1214251008 | bytes 10027008 | tf_op jit(solution)/shard_map/dot_general | solution.py:27
  14.5 0.0 all-reduce.2.cloned.1.call-update
  14.5 0.0 copy-done.4
  14.5 0.2 select_reduce_fusion
  14.7 66.8 %all-reduce.2.cloned.1.call-done = f32[24,16,384]{2,1,0:T(8,128)} async-done(((f32[24,16,384]{2,1,0:T(8,128)}), f32[24,16,384]{2,1,0:T(8,128)}) %all-reduce.2.cloned.1.call-update) | async-done | bytes 589840 | tf_op jit(solution)/shard_map/psum | solution.py:32
  81.6 2.2 multiply_add_fusion
  83.7 0.9 fusion.9
  84.6 0.0 copy-start.2
  84.7 0.0 copy-start.3
  84.7 2.1 copy.14
  86.7 9.9 %all-to-all-start = ((f32[32,2,16,384]{3,2,1,0:T(8,128)}), f32[32,2,16,384]{3,2,1,0:T(8,128)}, u32[]{:S(2)}, u32[]{:S(2)}) async-start(f32[32,2,16,384]{3,2,1,0:T(8,128)} %copy.14), calls=%async_computation | async-start | bytes 3145728 | tf_op jit(solution)/shard_map/all_to_all | solution.py:53
  96.7 0.7 fusion.18
  98.0 0.0 copy-done.2
  98.0 0.0 copy-done.3
  98.0 0.2 fusion.7
  98.2 38.5 %all-to-all-done = f32[32,2,16,384]{3,2,1,0:T(8,128)} async-done(((f32[32,2,16,384]{3,2,1,0:T(8,128)}), f32[32,2,16,384]{3,2,1,0:T(8,128)}, u32[]{:S(2)}, u32[]{:S(2)}) %all-to-all-start) | async-done | bytes 1572896 | tf_op jit(solution)/shard_map/all_to_all | solution.py:53
  136.7 2.4 multiply_reduce_fusion
  139.8 0.2 fusion.8
  140.0 1.6 multiply_convert_fusion
  141.6 4.8 %convolution_convert_fusion.1 = bf16[1024,4096]{1,0:T(8,128)(2,1)S(1)} fusion(bf16[1024,384]{1,0:T(8,128)(2,1)S(1)} %bitcast.56, bf16[4096,384]{1,0:T(8,128)(2,1)S(1)} %copy-done), kind=kOutput, calls=%fused_computation.4 | convolution fusion | flops 3225419776 | bytes 12320768 | tf_op jit(solution)/shard_map/dot_general | solution.py:12
  146.4 192.3 %all_to_all.10 = bf16[32,2,16,4096]{3,2,1,0:T(8,128)(2,1)} all-to-all(bf16[32,2,16,4096]{3,2,1,0:T(8,128)(2,1)S(1)} %bitcast.54), channel_id=1, replica_groups=mesh['replica'=8,'fsdp'=32] {'fsdp'}, dimensions={0} | all-to-all | bytes 16777216 | tf_op jit(solution)/shard_map/all_to_all | solution.py:65
  338.8 12.0 %copy.18 = bf16[8,8,16,4096]{3,1,2,0:T(8,128)(2,1)} copy(bf16[8,8,16,4096]{3,2,1,0:T(8,128)(2,1)} %bitcast.52) | data formatting | bytes 16777216
  350.7 4.7 %fusion = f32[24,65536]{1,0:T(8,128)S(1)} fusion(bf16[64,65536]{1,0:T(8,128)(2,1)} %bitcast.51, s32[24]{0:T(128)S(1)} %convert_add_fusion), kind=kOutput, calls=%fused_computation.1 | convolution fusion | flops 204476928 | bytes 14680160 | tf_op jit(solution)/shard_map/dot_general | solution.py:67
  355.4 0.0 copy-start.1
  355.4 3.6 copy.19
  359.0 0.0 copy-done.1
  359.0 2.6 fusion.2
  (4 shorter events, 0.0 us)
Async XLA Ops:
  7.2 1.9 copy-start
  7.2 7.4 %copy-start.4 = (s32[24]{0:T(128)S(1)}, s32[24]{0:T(128)}, u32[]{:S(2)}) copy-start(s32[24]{0:T(128)} %param.12) | copy-start | bytes 292
  7.2 74.4 %all-reduce.2.cloned.1.call-start = ((), (), s32[]{:S(2)}) async-start(), calls=%async_computation.2 | async-start | bytes 1179648 | tf_op jit(solution)/shard_map/psum | solution.py:32
  84.6 13.3 %copy-start.2 = (s32[24,2]{0,1:T(2,128)S(1)}, s32[24,2]{0,1:T(2,128)}, u32[]{:S(2)}) copy-start(s32[24,2]{0,1:T(2,128)} %param.13) | copy-start | bytes 580
  84.7 13.4 %copy-start.3 = (f32[4,6]{1,0:T(4,128)S(1)}, f32[4,6]{1,0:T(4,128)}, u32[]{:S(2)}) copy-start(f32[4,6]{1,0:T(4,128)} %param.11) | copy-start | bytes 292
  86.7 50.0 %all-to-all-start = ((f32[32,2,16,384]{3,2,1,0:T(8,128)}), f32[32,2,16,384]{3,2,1,0:T(8,128)}, u32[]{:S(2)}, u32[]{:S(2)}) async-start(f32[32,2,16,384]{3,2,1,0:T(8,128)} %copy.14), calls=%async_computation | async-start | bytes 3145728 | tf_op jit(solution)/shard_map/all_to_all | solution.py:53
  355.4 3.7 copy-start.1
Sparse Core Ops, SparseCore 0:
  14.7 66.8 all-reduce.1
where the time goes:
time: 369 us
  blocking collectives  192 us (52%)
  waiting for transfers between devices  105 us (28%)
  local copies, waits for them, and re-layouts  19.5 us (5%)
  matrix products  16.2 us (4%)
  between operations  15.5 us (4%)
  starting transfers between devices  9.97 us (3%)
  other arithmetic  9.73 us (3%)
    all_to_all x1, blocking collectives, local(): lax.all_to_all(slot_update, 'fsdp', split_axis=0, concat_axis=0, tiled=True)  192 us
    psum x1, waiting for transfers between devices, local(): lax.psum(compressed.reshape(matrices, rows_dev, rank_dim), 'replica')  66.8 us
    all_to_all x1, waiting for transfers between devices, local(): lax.all_to_all(outgoing, 'fsdp', split_axis=0, concat_axis=0, tiled=True)  38.5 us
    unnamed x12, local copies, waits for them, and re-layouts  17.5 us
    all_to_all x1, starting transfers between devices, local(): lax.all_to_all(outgoing, 'fsdp', split_axis=0, concat_axis=0, tiled=True)  9.93 us
  transfers between devices with their start and end apart: 2, of which 2 were waited for; matrix products, arithmetic and copies ran while one was open for 0% of the time, Pallas kernels for 0%

commit v1 on v0

v1 whole, which is shorter than its diff:
```python
import jax
import jax.numpy as jnp
from jax import lax
from jax.sharding import PartitionSpec as P

OUTER_MOMENTUM = 0.9
EPSILON = 1e-06


def local(anchor_params, replica_params, projection, momentum, rate_table, owner_list, layer_kind):
    matrices, rows_dev, model_width = anchor_params.shape
    rank_dim = projection.shape[1]
    all_rows = rows_dev * lax.axis_size("fsdp")
    highest = lax.Precision.HIGHEST
    pseudo_grad = (
        anchor_params.astype(jnp.float32) - replica_params[0].astype(jnp.float32)
    ).astype(jnp.bfloat16)
    compressed = jnp.dot(
        pseudo_grad.reshape(matrices * rows_dev, model_width),
        projection,
        preferred_element_type=jnp.float32,
    )
    summed = lax.psum(compressed.reshape(matrices, rows_dev, rank_dim), "replica")
    outer_grad = summed / lax.axis_size("replica")
    new_momentum = OUTER_MOMENTUM * momentum + outer_grad
    outer_step = outer_grad + OUTER_MOMENTUM * new_momentum
    squares = lax.psum(jnp.sum(outer_step * outer_step, axis=(1, 2)), "fsdp")
    same_group = (owner_list[:, None] == owner_list[None, :]).astype(jnp.float32)
    group_squares = jnp.dot(same_group, squares, precision=highest)
    group_count = jnp.sum(same_group, axis=1)
    scaling = lax.rsqrt(group_squares / (group_count * (all_rows * rank_dim)) + EPSILON)
    outer_rate = rate_table[layer_kind[:, 0], layer_kind[:, 1]]
    direction = (outer_step * (outer_rate * scaling)[:, None, None]).astype(jnp.bfloat16)
    update = lax.dot_general(
        direction.reshape(matrices * rows_dev, rank_dim),
        projection,
        (((1,), (1,)), ((), ())),
        preferred_element_type=jnp.float32,
    ).astype(jnp.bfloat16)
    new_params = (
        anchor_params.astype(jnp.float32)
        - update.reshape(matrices, rows_dev, model_width).astype(jnp.float32)
    ).astype(jnp.bfloat16)
    return (new_params, new_momentum)


def solution(mesh):
    placed = (
        P(None, "fsdp", None),
        P("replica", None, "fsdp", None),
        P(),
        P(None, "fsdp", None),
        P(),
        P(),
        P(),
    )
    return jax.shard_map(
        local,
        mesh=mesh,
        in_specs=placed,
        out_specs=(P(None, "fsdp", None), P(None, "fsdp", None)),
        check_vma=False,
    )
```

time: 369 us -> 173 us (0.47)
  blocking collectives: 192 us -> 75 us
  waiting for transfers between devices: 105 us -> 66 us
  local copies, waits for them, and re-layouts: 19.5 us -> 2.71 us
  starting transfers between devices: 9.97 us -> 0.04 us
  matrix products: 16.2 us -> 7.48 us
    all_to_all x1 -> x0, blocking collectives: 192 us -> none  [local(): lax.all_to_all(slot_update, 'fsdp', split_axis=0, concat_axis=0, tiled=True)]
    psum x0 -> x1, blocking collectives: none -> 75 us  [local(): squares = lax.psum(jnp.sum(outer_step * outer_step, axis=(1, 2)), 'fsdp')]
    all_to_all x1 -> x0, waiting for transfers between devices: 38.5 us -> none  [local(): lax.all_to_all(outgoing, 'fsdp', split_axis=0, concat_axis=0, tiled=True)]
    unnamed x12 -> x10, local copies, waits for them, and re-layouts: 17.5 us -> 1.86 us
    all_to_all x1 -> x0, starting transfers between devices: 9.93 us -> none  [local(): lax.all_to_all(outgoing, 'fsdp', split_axis=0, concat_axis=0, tiled=True)]
    dot_general x5 -> x2, matrix products: 10.7 us -> 2.03 us  [the longest x1 1.84 us: local(): lax.dot_general(direction.reshape(matrices * rows_dev, rank_dim), project...]
  transfers between devices with their start and end apart: 2 -> 1, of which waited for: 2 -> 1; matrix products, arithmetic and copies ran while one was open for 0% -> 1% of each run, Pallas kernels for 0% -> 0%
where the time goes in v1:
time: 173 us; the launch traced here: 172 us
  blocking collectives  75 us (43%)
  waiting for transfers between devices  66 us (38%)
  between operations  14.1 us (8%)
  matrix products  7.48 us (4%)
  other arithmetic  6.67 us (4%)
  local copies, waits for them, and re-layouts  2.71 us (2%)
    psum x1, blocking collectives, local(): squares = lax.psum(jnp.sum(outer_step * outer_step, axis=(1, 2)), 'fsdp')  75 us
    psum x1, waiting for transfers between devices, local(): lax.psum(compressed.reshape(matrices, rows_dev, rank_dim), 'replica')  66 us
    dot_general x1, matrix products, local(): jnp.dot(pseudo_grad.reshape(matrices * rows_dev, model_width), projection...  5.45 us
  transfers between devices with their start and end apart: 1, of which 1 were waited for; matrix products, arithmetic and copies ran while one was open for 1% of the time, Pallas kernels for 0%

profile of v1, /device:TPU:24, one launch (start us, length us, event | category | flops | bytes accessed | tf_op | source)
XLA Modules:
  0.0 172.0 jit_solution(15849342084656338026)
XLA Ops:
  7.2 0.0 copy-start
  7.2 0.0 copy-start.3
  7.2 0.0 copy-start.1
  7.2 0.0 copy-start.4
  7.2 0.0 all-reduce.2.cloned.1.call-start
  7.3 1.8 %copy-done = bf16[4096,384]{1,0:T(8,128)(2,1)S(1)} copy-done((bf16[4096,384]{1,0:T(8,128)(2,1)S(1)}, bf16[4096,384]{1,0:T(8,128)(2,1)}, u32[]{:S(2)}) %copy-start) | copy-done | bytes 3145752
  9.1 5.5 %fusion.2 = f32[24,16,384]{2,1,0:T(8,128)} fusion(bf16[24,16,4096]{2,1,0:T(8,128)(2,1)} %param.7, bf16[1,24,16,4096]{3,2,1,0:T(8,128)(2,1)} %param.8, bf16[4096,384]{1,0:T(8,128)(2,1)S(1)} %copy-done), kind=kOutput, calls=%fused_computation.6 | convolution fusion | flops 1214251008 | bytes 10027008 | tf_op jit(solution)/shard_map/dot_general | solution.py:18
  14.5 0.0 all-reduce.2.cloned.1.call-update
  14.5 0.0 copy-done.3
  14.6 0.0 copy-done.1
  14.6 0.8 gather_fusion
  15.4 0.0 copy-done.4
  15.4 0.2 fusion.11
  15.6 66.0 %all-reduce.2.cloned.1.call-done = f32[24,16,384]{2,1,0:T(8,128)} async-done(((f32[24,16,384]{2,1,0:T(8,128)}), f32[24,16,384]{2,1,0:T(8,128)}) %all-reduce.2.cloned.1.call-update) | async-done | bytes 589840 | tf_op jit(solution)/shard_map/psum | solution.py:23
  81.6 2.2 %multiply_reduce_fusion = (f32[24]{0:T(128)S(1)}, f32[24,16,384]{2,1,0:T(8,128)}) fusion(f32[24,16,384]{2,1,0:T(8,128)} %all-reduce.2.cloned.1.call-done, f32[24,16,384]{2,1,0:T(8,128)} %param.10), kind=kLoop, calls=%fused_computation.15 | loop fusion | flops 1032168 | bytes 1769568 | tf_op jit(solution)/shard_map/reduce_sum | solution.py:27
  83.8 75.0 %psum.15 = f32[24]{0:T(128)S(1)} all-reduce(f32[24]{0:T(128)S(1)} %get-tuple-element.2), channel_id=1, replica_groups=mesh['replica'=8,'fsdp'=32] {'fsdp'}, use_global_device_ids=true, to_apply=%region_2.0 | all-reduce | flops 24 | bytes 192 | tf_op jit(solution)/shard_map/psum | solution.py:27
  158.8 0.2 fusion.9
  159.0 1.4 multiply_convert_fusion
  160.4 0.0 copy-start.2
  160.4 1.8 %convolution_convert_fusion = bf16[384,4096]{1,0:T(8,128)(2,1)S(1)} fusion(bf16[384,384]{1,0:T(8,128)(2,1)S(1)} %bitcast.30, bf16[4096,384]{1,0:T(8,128)(2,1)S(1)} %copy-done), kind=kOutput, calls=%fused_computation.5 | convolution fusion | flops 1209532416 | bytes 6586368 | tf_op jit(solution)/shard_map/dot_general | solution.py:34
  162.3 0.0 copy-done.2
  162.3 2.9 %fusion.1 = bf16[24,16,4096]{2,1,0:T(8,128)(2,1)} fusion(bf16[24,16,4096]{2,1,0:T(8,128)(2,1)S(1)} %copy-done.2, bf16[24,16,4096]{2,1,0:T(8,128)(2,1)S(1)} %bitcast.29), kind=kLoop, calls=%fused_computation.4 | loop fusion | flops 6291456 | bytes 9437184 | tf_op jit(solution)/shard_map/convert_element_type | solution.py:43
  (1 shorter events, 0.0 us)
Async XLA Ops:
  7.2 1.9 %copy-start = (bf16[4096,384]{1,0:T(8,128)(2,1)S(1)}, bf16[4096,384]{1,0:T(8,128)(2,1)}, u32[]{:S(2)}) copy-start(bf16[4096,384]{1,0:T(8,128)(2,1)} %param.9) | copy-start | bytes 9437188
  7.2 7.4 %copy-start.3 = (s32[24,2]{0,1:T(2,128)S(1)}, s32[24,2]{0,1:T(2,128)}, u32[]{:S(2)}) copy-start(s32[24,2]{0,1:T(2,128)} %param.13) | copy-start | bytes 580
  7.2 7.4 %copy-start.1 = (f32[4,6]{1,0:T(4,128)S(1)}, f32[4,6]{1,0:T(4,128)}, u32[]{:S(2)}) copy-start(f32[4,6]{1,0:T(4,128)} %param.11) | copy-start | bytes 292
  7.2 8.2 %copy-start.4 = (s32[24]{0:T(128)S(1)}, s32[24]{0:T(128)}, u32[]{:S(2)}) copy-start(s32[24]{0:T(128)} %param.12) | copy-start | bytes 292
  7.2 74.4 %all-reduce.2.cloned.1.call-start = ((), (), s32[]{:S(2)}) async-start(), calls=%async_computation | async-start | bytes 1179648 | tf_op jit(solution)/shard_map/psum | solution.py:23
  160.4 1.9 %copy-start.2 = (bf16[24,16,4096]{2,1,0:T(8,128)(2,1)S(1)}, bf16[24,16,4096]{2,1,0:T(8,128)(2,1)}, u32[]{:S(2)}) copy-start(bf16[24,16,4096]{2,1,0:T(8,128)(2,1)} %param.7) | copy-start | bytes 9437188
Sparse Core Ops, SparseCore 0:
  14.7 66.8 all-reduce.1

commit v2 on v1

--- a/solution.py
+++ b/solution.py
@@ -5,6 +5,15 @@
 
 OUTER_MOMENTUM = 0.9
 EPSILON = 1e-06
+
+def butterfly(x, axis):
+    size = lax.axis_size(axis)
+    step = 1
+    while step < size:
+        perm = [(i, i ^ step) for i in range(size)]
+        x = x + lax.ppermute(x, axis, perm)
+        step *= 2
+    return x
 
 
 def local(anchor_params, replica_params, projection, momentum, rate_table, owner_list, layer_kind):
@@ -20,11 +29,11 @@
         projection,
         preferred_element_type=jnp.float32,
     )
-    summed = lax.psum(compressed.reshape(matrices, rows_dev, rank_dim), "replica")
+    summed = butterfly(compressed.reshape(matrices, rows_dev, rank_dim), "replica")
     outer_grad = summed / lax.axis_size("replica")
     new_momentum = OUTER_MOMENTUM * momentum + outer_grad
     outer_step = outer_grad + OUTER_MOMENTUM * new_momentum
-    squares = lax.psum(jnp.sum(outer_step * outer_step, axis=(1, 2)), "fsdp")
+    squares = butterfly(jnp.sum(outer_step * outer_step, axis=(1, 2)), "fsdp")
     same_group = (owner_list[:, None] == owner_list[None, :]).astype(jnp.float32)
     group_squares = jnp.dot(same_group, squares, precision=highest)
     group_count = jnp.sum(same_group, axis=1)

time: 173 us -> 74.2 us (0.43)
  blocking collectives: 75 us -> 0 us
  waiting for transfers between devices: 66 us -> 38.8 us
  starting transfers between devices: 0.04 us -> 19.2 us
  between operations: 14.1 us -> 0.74 us
    psum x1 -> x0, blocking collectives: 75 us -> none  [local(): squares = lax.psum(jnp.sum(outer_step * outer_step, axis=(1, 2)), 'fsdp')]
    psum x1 -> x0, waiting for transfers between devices: 66 us -> none  [local(): lax.psum(compressed.reshape(matrices, rows_dev, rank_dim), 'replica')]
    ppermute x0 -> x8, waiting for transfers between devices: none -> 38.8 us  [butterfly(): x = x + lax.ppermute(x, axis, perm)]
    ppermute x0 -> x8, starting transfers between devices: none -> 19.2 us  [butterfly(): x = x + lax.ppermute(x, axis, perm)]
  transfers between devices with their start and end apart: 1 -> 8, of which waited for: 1 -> 8; matrix products, arithmetic and copies ran while one was open for 1% -> 1% of each run, Pallas kernels for 0% -> 0%
where the time goes in v2:
time: 74.2 us; the launch traced here: 74 us
  waiting for transfers between devices  38.8 us (52%)
  starting transfers between devices  19.2 us (26%)
  matrix products  6.64 us (9%)
  other arithmetic  5.81 us (8%)
  local copies, waits for them, and re-layouts  2.82 us (4%)
    ppermute x8, waiting for transfers between devices, butterfly(): x = x + lax.ppermute(x, axis, perm)  38.8 us
    ppermute x8, starting transfers between devices, butterfly(): x = x + lax.ppermute(x, axis, perm)  19.2 us
    dot_general x1, matrix products, local(): jnp.dot(pseudo_grad.reshape(matrices * rows_dev, model_width), projection...  4.63 us
    convert_element_type x1, other arithmetic, local(): new_params = (anchor_params.astype(jnp.float32) - update.reshape(matrices...  2.87 us
    unnamed x16, local copies, waits for them, and re-layouts  1.98 us
    dot_general x1, matrix products, local(): lax.dot_general(direction.reshape(matrices * rows_dev, rank_dim), project...  1.82 us
    convert_element_type x1, other arithmetic, local(): (outer_step * (outer_rate * scaling)[:, None, None]).astype(jnp.bfloat16)  1.57 us
  transfers between devices with their start and end apart: 8, of which 8 were waited for; matrix products, arithmetic and copies ran while one was open for 1% of the time, Pallas kernels for 0%

profile of v2, /device:TPU:24, one launch (start us, length us, event | category | flops | bytes accessed | tf_op | source)
XLA Modules:
  0.0 74.0 jit_solution(9517340756051171071)
XLA Ops:
  0.6 0.0 copy-start
  0.6 1.9 %copy-done = bf16[4096,384]{1,0:T(8,128)(2,1)S(1)} copy-done((bf16[4096,384]{1,0:T(8,128)(2,1)S(1)}, bf16[4096,384]{1,0:T(8,128)(2,1)}, u32[]{:S(2)}) %copy-start) | copy-done | bytes 3145752
  2.5 4.6 %fusion.2 = f32[24,16,384]{2,1,0:T(8,128)S(1)} fusion(bf16[24,16,4096]{2,1,0:T(8,128)(2,1)} %param.7, bf16[1,24,16,4096]{3,2,1,0:T(8,128)(2,1)} %param.8, bf16[4096,384]{1,0:T(8,128)(2,1)S(1)} %copy-done), kind=kOutput, calls=%fused_computation.6 | convolution fusion | flops 1214251008 | bytes 10027008 | tf_op jit(solution)/shard_map/dot_general | solution.py:27
  7.2 0.0 copy-start.5
  7.2 0.0 copy-start.6
  7.2 0.0 copy-start.1
  7.2 0.1 collective-permute-start
  7.3 2.0 %collective-permute-done = f32[24,16,384]{2,1,0:T(8,128)S(1)} collective-permute-done((f32[24,16,384]{2,1,0:T(8,128)S(1)}, f32[24,16,384]{2,1,0:T(8,128)S(1)}, u32[]{:S(2)}, u32[]{:S(2)}) %collective-permute-start) | collective-permute-done | bytes 589856 | tf_op jit(solution)/shard_map/ppermute | solution.py:14
  9.3 0.1 add.41
  9.4 0.8 %collective-permute-start.1 = (f32[24,16,384]{2,1,0:T(8,128)S(1)}, f32[24,16,384]{2,1,0:T(8,128)S(1)}, u32[]{:S(2)}, u32[]{:S(2)}) collective-permute-start(f32[24,16,384]{2,1,0:T(8,128)S(1)} %add.41), channel_id=1, source_target_pairs={{0,64},{32,96},{64,0},{96,32},{128,192},{160,224},{192,128},{224,1... | collective-permute-start | bytes 1769480 | tf_op jit(solution)/shard_map/ppermute | solution.py:14
  10.2 14.6 %collective-permute-done.1 = f32[24,16,384]{2,1,0:T(8,128)S(1)} collective-permute-done((f32[24,16,384]{2,1,0:T(8,128)S(1)}, f32[24,16,384]{2,1,0:T(8,128)S(1)}, u32[]{:S(2)}, u32[]{:S(2)}) %collective-permute-start.1) | collective-permute-done | bytes 589856 | tf_op jit(solution)/shard_map/ppermute | solution.py:14
  24.8 0.1 add.42
  24.9 1.7 %collective-permute-start.2 = (f32[24,16,384]{2,1,0:T(8,128)S(1)}, f32[24,16,384]{2,1,0:T(8,128)S(1)}, u32[]{:S(2)}, u32[]{:S(2)}) collective-permute-start(f32[24,16,384]{2,1,0:T(8,128)S(1)} %add.42), channel_id=1, source_target_pairs={{0,128},{32,160},{64,192},{96,224},{128,0},{160,32},{192,64},{224,... | collective-permute-start | bytes 1769480 | tf_op jit(solution)/shard_map/ppermute | solution.py:14
  26.7 14.4 %collective-permute-done.2 = f32[24,16,384]{2,1,0:T(8,128)S(1)} collective-permute-done((f32[24,16,384]{2,1,0:T(8,128)S(1)}, f32[24,16,384]{2,1,0:T(8,128)S(1)}, u32[]{:S(2)}, u32[]{:S(2)}) %collective-permute-start.2) | collective-permute-done | bytes 589856 | tf_op jit(solution)/shard_map/ppermute | solution.py:14
  41.0 1.0 %multiply_reduce_fusion = (f32[24]{0:T(128)S(1)}, f32[24,16,384]{2,1,0:T(8,128)}) fusion(f32[24,16,384]{2,1,0:T(8,128)S(1)} %add.42, f32[24,16,384]{2,1,0:T(8,128)S(1)} %collective-permute-done.2, f32[24,16,384]{2,1,0:T(8,128)S(1)} %copy-done.5), kind=kLoop, calls=%fused_computation.15 | loop fusion | flops 1179624 | bytes 2359392 | tf_op jit(solution)/shard_map/reduce_sum | solution.py:36
  42.1 1.9 %collective-permute-start.3 = (f32[24]{0:T(128)S(1)}, f32[24]{0:T(128)S(1)}, u32[]{:S(2)}, u32[]{:S(2)}) collective-permute-start(f32[24]{0:T(128)S(1)} %get-tuple-element.2), channel_id=1, source_target_pairs={{0,1},{1,0},{2,3},{3,2},{4,5},{5,4},{6,7},{7,6},{8,9},{9,8},{10,11... | collective-permute-start | bytes 296 | tf_op jit(solution)/shard_map/ppermute | solution.py:14
  44.0 1.7 %collective-permute-done.3 = f32[24]{0:T(128)S(1)} collective-permute-done((f32[24]{0:T(128)S(1)}, f32[24]{0:T(128)S(1)}, u32[]{:S(2)}, u32[]{:S(2)}) %collective-permute-start.3) | collective-permute-done | bytes 128 | tf_op jit(solution)/shard_map/ppermute | solution.py:14
  45.6 3.3 %collective-permute-start.4 = (f32[24]{0:T(128)S(1)}, f32[24]{0:T(128)S(1)}, u32[]{:S(2)}, u32[]{:S(2)}) collective-permute-start(f32[24]{0:T(128)S(1)} %add.48), channel_id=1, source_target_pairs={{0,2},{1,3},{2,0},{3,1},{4,6},{5,7},{6,4},{7,5},{8,10},{9,11},{10,... | collective-permute-start | bytes 296 | tf_op jit(solution)/shard_map/ppermute | solution.py:14
  48.9 1.5 %collective-permute-done.4 = f32[24]{0:T(128)S(1)} collective-permute-done((f32[24]{0:T(128)S(1)}, f32[24]{0:T(128)S(1)}, u32[]{:S(2)}, u32[]{:S(2)}) %collective-permute-start.4) | collective-permute-done | bytes 128 | tf_op jit(solution)/shard_map/ppermute | solution.py:14
  50.4 6.8 %collective-permute-start.5 = (f32[24]{0:T(128)S(1)}, f32[24]{0:T(128)S(1)}, u32[]{:S(2)}, u32[]{:S(2)}) collective-permute-start(f32[24]{0:T(128)S(1)} %add.49), channel_id=1, source_target_pairs={{0,4},{1,5},{2,6},{3,7},{4,0},{5,1},{6,2},{7,3},{8,12},{9,13},{10,... | collective-permute-start | bytes 296 | tf_op jit(solution)/shard_map/ppermute | solution.py:14
  57.3 1.5 %collective-permute-done.5 = f32[24]{0:T(128)S(1)} collective-permute-done((f32[24]{0:T(128)S(1)}, f32[24]{0:T(128)S(1)}, u32[]{:S(2)}, u32[]{:S(2)}) %collective-permute-start.5) | collective-permute-done | bytes 128 | tf_op jit(solution)/shard_map/ppermute | solution.py:14
  58.8 1.5 %collective-permute-start.6 = (f32[24]{0:T(128)S(1)}, f32[24]{0:T(128)S(1)}, u32[]{:S(2)}, u32[]{:S(2)}) collective-permute-start(f32[24]{0:T(128)S(1)} %add.50), channel_id=1, source_target_pairs={{0,8},{1,9},{2,10},{3,11},{4,12},{5,13},{6,14},{7,15},{8,0},{9,1},... | collective-permute-start | bytes 296 | tf_op jit(solution)/shard_map/ppermute | solution.py:14
  60.3 0.2 fusion.11
  60.5 1.9 %collective-permute-done.6 = f32[24]{0:T(128)S(1)} collective-permute-done((f32[24]{0:T(128)S(1)}, f32[24]{0:T(128)S(1)}, u32[]{:S(2)}, u32[]{:S(2)}) %collective-permute-start.6) | collective-permute-done | bytes 128 | tf_op jit(solution)/shard_map/ppermute | solution.py:14
  62.4 3.0 %collective-permute-start.7 = (f32[24]{0:T(128)S(1)}, f32[24]{0:T(128)S(1)}, u32[]{:S(2)}, u32[]{:S(2)}) collective-permute-start(f32[24]{0:T(128)S(1)} %add.51), channel_id=1, source_target_pairs={{0,16},{1,17},{2,18},{3,19},{4,20},{5,21},{6,22},{7,23},{8,24},{9,... | collective-permute-start | bytes 296 | tf_op jit(solution)/shard_map/ppermute | solution.py:14
  65.4 0.8 %gather_fusion = f32[24]{0:T(128)S(1)} fusion(f32[4,6]{1,0:T(4,128)S(1)} %copy-done.1, s32[24]{0:T(128)S(1)} %fusion.19), kind=kCustom, calls=%fused_computation | custom fusion | bytes 384 | tf_op jit(solution)/shard_map/gather | solution.py:41
  66.3 1.2 %collective-permute-done.7 = f32[24]{0:T(128)S(1)} collective-permute-done((f32[24]{0:T(128)S(1)}, f32[24]{0:T(128)S(1)}, u32[]{:S(2)}, u32[]{:S(2)}) %collective-permute-start.7) | collective-permute-done | bytes 128 | tf_op jit(solution)/shard_map/ppermute | solution.py:14
  67.5 0.2 fusion.9
  67.7 1.6 %multiply_convert_fusion = bf16[24,16,384]{2,1,0:T(8,128)(2,1)S(1)} fusion(f32[24]{0:T(128)S(1)} %fusion.9, f32[24,16,384]{2,1,0:T(8,128)} %get-tuple-element.3, f32[24,16,384]{2,1,0:T(8,128)} %copy-done.2, f32[24,16,384]{2,1,0:T(8,128)} %copy-done.4), kind=kLoop, calls=%fused_computation.14 | loop fusion | flops 884736 | bytes 2064480 | tf_op jit(solution)/shard_map/convert_element_type | solution.py:42
  69.3 1.8 %convolution_convert_fusion = bf16[384,4096]{1,0:T(8,128)(2,1)S(1)} fusion(bf16[384,384]{1,0:T(8,128)(2,1)S(1)} %bitcast.30, bf16[4096,384]{1,0:T(8,128)(2,1)S(1)} %copy-done), kind=kOutput, calls=%fused_computation.5 | convolution fusion | flops 1209532416 | bytes 6586368 | tf_op jit(solution)/shard_map/dot_general | solution.py:43
  71.1 0.0 copy-done.3
  71.1 2.9 %fusion.1 = bf16[24,16,4096]{2,1,0:T(8,128)(2,1)} fusion(bf16[24,16,4096]{2,1,0:T(8,128)(2,1)S(1)} %copy-done.3, bf16[24,16,4096]{2,1,0:T(8,128)(2,1)S(1)} %bitcast.29), kind=kLoop, calls=%fused_computation.4 | loop fusion | flops 6291456 | bytes 9437184 | tf_op jit(solution)/shard_map/convert_element_type | solution.py:52
  (15 shorter events, 0.0 us)
Async XLA Ops:
  0.6 1.9 %copy-start = (bf16[4096,384]{1,0:T(8,128)(2,1)S(1)}, bf16[4096,384]{1,0:T(8,128)(2,1)}, u32[]{:S(2)}) copy-start(bf16[4096,384]{1,0:T(8,128)(2,1)} %param.9) | copy-start | bytes 9437188
  7.2 33.9 %copy-start.5 = (f32[24,16,384]{2,1,0:T(8,128)S(1)}, f32[24,16,384]{2,1,0:T(8,128)}, u32[]{:S(2)}) copy-start(f32[24,16,384]{2,1,0:T(8,128)} %param.10) | copy-start | bytes 1769476
  7.2 50.1 %copy-start.6 = (s32[24,2]{0,1:T(2,128)S(1)}, s32[24,2]{0,1:T(2,128)}, u32[]{:S(2)}) copy-start(s32[24,2]{0,1:T(2,128)} %param.13) | copy-start | bytes 580
  7.2 53.1 %copy-start.7 = (s32[24]{0:T(128)S(1)}, s32[24]{0:T(128)}, u32[]{:S(2)}) copy-start(s32[24]{0:T(128)} %param.12) | copy-start | bytes 292
  7.2 58.2 %copy-start.1 = (f32[4,6]{1,0:T(4,128)S(1)}, f32[4,6]{1,0:T(4,128)}, u32[]{:S(2)}) copy-start(f32[4,6]{1,0:T(4,128)} %param.11) | copy-start | bytes 292
  7.2 2.1 %collective-permute-start = (f32[24,16,384]{2,1,0:T(8,128)S(1)}, f32[24,16,384]{2,1,0:T(8,128)S(1)}, u32[]{:S(2)}, u32[]{:S(2)}) collective-permute-start(f32[24,16,384]{2,1,0:T(8,128)S(1)} %fusion.2), channel_id=1, source_target_pairs={{0,32},{32,0},{64,96},{96,64},{128,160},{160,128},{192,224},{224,1... | collective-permute-start | bytes 1769480 | tf_op jit(solution)/shard_map/ppermute | solution.py:14
  9.4 15.5 %collective-permute-start.1 = (f32[24,16,384]{2,1,0:T(8,128)S(1)}, f32[24,16,384]{2,1,0:T(8,128)S(1)}, u32[]{:S(2)}, u32[]{:S(2)}) collective-permute-start(f32[24,16,384]{2,1,0:T(8,128)S(1)} %add.41), channel_id=1, source_target_pairs={{0,64},{32,96},{64,0},{96,32},{128,192},{160,224},{192,128},{224,1... | collective-permute-start | bytes 1769480 | tf_op jit(solution)/shard_map/ppermute | solution.py:14
  24.9 16.1 %copy-start.2 = (f32[24,16,384]{2,1,0:T(8,128)}, f32[24,16,384]{2,1,0:T(8,128)S(1)}, u32[]{:S(2)}) copy-start(f32[24,16,384]{2,1,0:T(8,128)S(1)} %add.42) | copy-start | bytes 1769476
  24.9 16.1 %collective-permute-start.2 = (f32[24,16,384]{2,1,0:T(8,128)S(1)}, f32[24,16,384]{2,1,0:T(8,128)S(1)}, u32[]{:S(2)}, u32[]{:S(2)}) collective-permute-start(f32[24,16,384]{2,1,0:T(8,128)S(1)} %add.42), channel_id=1, source_target_pairs={{0,128},{32,160},{64,192},{96,224},{128,0},{160,32},{192,64},{224,... | collective-permute-start | bytes 1769480 | tf_op jit(solution)/shard_map/ppermute | solution.py:14
  41.0 1.0 %copy-start.4 = (f32[24,16,384]{2,1,0:T(8,128)}, f32[24,16,384]{2,1,0:T(8,128)S(1)}, u32[]{:S(2)}) copy-start(f32[24,16,384]{2,1,0:T(8,128)S(1)} %collective-permute-done.2) | copy-start | bytes 1769476
  42.1 3.6 %collective-permute-start.3 = (f32[24]{0:T(128)S(1)}, f32[24]{0:T(128)S(1)}, u32[]{:S(2)}, u32[]{:S(2)}) collective-permute-start(f32[24]{0:T(128)S(1)} %get-tuple-element.2), channel_id=1, source_target_pairs={{0,1},{1,0},{2,3},{3,2},{4,5},{5,4},{6,7},{7,6},{8,9},{9,8},{10,11... | collective-permute-start | bytes 296 | tf_op jit(solution)/shard_map/ppermute | solution.py:14
  45.6 4.8 %collective-permute-start.4 = (f32[24]{0:T(128)S(1)}, f32[24]{0:T(128)S(1)}, u32[]{:S(2)}, u32[]{:S(2)}) collective-permute-start(f32[24]{0:T(128)S(1)} %add.48), channel_id=1, source_target_pairs={{0,2},{1,3},{2,0},{3,1},{4,6},{5,7},{6,4},{7,5},{8,10},{9,11},{10,... | collective-permute-start | bytes 296 | tf_op jit(solution)/shard_map/ppermute | solution.py:14
  50.4 8.4 %collective-permute-start.5 = (f32[24]{0:T(128)S(1)}, f32[24]{0:T(128)S(1)}, u32[]{:S(2)}, u32[]{:S(2)}) collective-permute-start(f32[24]{0:T(128)S(1)} %add.49), channel_id=1, source_target_pairs={{0,4},{1,5},{2,6},{3,7},{4,0},{5,1},{6,2},{7,3},{8,12},{9,13},{10,... | collective-permute-start | bytes 296 | tf_op jit(solution)/shard_map/ppermute | solution.py:14
  58.8 3.6 %collective-permute-start.6 = (f32[24]{0:T(128)S(1)}, f32[24]{0:T(128)S(1)}, u32[]{:S(2)}, u32[]{:S(2)}) collective-permute-start(f32[24]{0:T(128)S(1)} %add.50), channel_id=1, source_target_pairs={{0,8},{1,9},{2,10},{3,11},{4,12},{5,13},{6,14},{7,15},{8,0},{9,1},... | collective-permute-start | bytes 296 | tf_op jit(solution)/shard_map/ppermute | solution.py:14
  62.4 5.1 %collective-permute-start.7 = (f32[24]{0:T(128)S(1)}, f32[24]{0:T(128)S(1)}, u32[]{:S(2)}, u32[]{:S(2)}) collective-permute-start(f32[24]{0:T(128)S(1)} %add.51), channel_id=1, source_target_pairs={{0,16},{1,17},{2,18},{3,19},{4,20},{5,21},{6,22},{7,23},{8,24},{9,... | collective-permute-start | bytes 296 | tf_op jit(solution)/shard_map/ppermute | solution.py:14
  69.3 1.9 %copy-start.3 = (bf16[24,16,4096]{2,1,0:T(8,128)(2,1)S(1)}, bf16[24,16,4096]{2,1,0:T(8,128)(2,1)}, u32[]{:S(2)}) copy-start(bf16[24,16,4096]{2,1,0:T(8,128)(2,1)} %param.7) | copy-start | bytes 9437188

commit v3 on v2

--- a/solution.py
+++ b/solution.py
@@ -16,6 +16,29 @@
     return x
 
 
+def replica_sum(x, axis):
+    size = lax.axis_size(axis)
+    chips = size // 2
+    if size % 2 or chips != 4:
+        return butterfly(x, axis)
+    core = lax.axis_index(axis) % 2
+    swap = [(i, i ^ 1) for i in range(size)]
+    half = x.shape[0] // 2
+    keep = lax.dynamic_slice_in_dim(x, core * half, half)
+    send = lax.dynamic_slice_in_dim(x, (1 - core) * half, half)
+    x = keep + lax.ppermute(send, axis, swap)
+    even = [(0, 1), (2, 3)]
+    odd = [(1, 2), (3, 0)]
+    for step in range(2):
+        perm = []
+        for c in range(2):
+            for a, b in (even if c == step else odd):
+                perm += [(a * 2 + c, b * 2 + c), (b * 2 + c, a * 2 + c)]
+        x = x + lax.ppermute(x, axis, perm)
+    other = lax.ppermute(x, axis, swap)
+    return jnp.where(core == 1, jnp.concatenate([other, x]), jnp.concatenate([x, other]))
+
+
 def local(anchor_params, replica_params, projection, momentum, rate_table, owner_list, layer_kind):
     matrices, rows_dev, model_width = anchor_params.shape
     rank_dim = projection.shape[1]
@@ -29,11 +52,11 @@
         projection,
         preferred_element_type=jnp.float32,
     )
-    summed = butterfly(compressed.reshape(matrices, rows_dev, rank_dim), "replica")
+    summed = replica_sum(compressed.reshape(matrices, rows_dev, rank_dim), "replica")
     outer_grad = summed / lax.axis_size("replica")
     new_momentum = OUTER_MOMENTUM * momentum + outer_grad
     outer_step = outer_grad + OUTER_MOMENTUM * new_momentum
-    squares = butterfly(jnp.sum(outer_step * outer_step, axis=(1, 2)), "fsdp")
+    squares = jnp.sum(lax.all_to_all(jnp.broadcast_to(jnp.sum(outer_step * outer_step, axis=(1, 2)), (lax.axis_size("fsdp"), outer_step.shape[0])), "fsdp", 0, 0, tiled=True), axis=0)
     same_group = (owner_list[:, None] == owner_list[None, :]).astype(jnp.float32)
     group_squares = jnp.dot(same_group, squares, precision=highest)
     group_count = jnp.sum(same_group, axis=1)

time: 74.2 us -> 58.9 us (0.79)
  waiting for transfers between devices: 38.8 us -> 24.1 us
  starting transfers between devices: 19.2 us -> 14.3 us
  local copies, waits for them, and re-layouts: 2.82 us -> 4.93 us
  other arithmetic: 5.81 us -> 7.88 us
    ppermute x8 -> x4, waiting for transfers between devices: 38.8 us -> 15.4 us  [the longest x2 12 us: replica_sum(): x = x + lax.ppermute(x, axis, perm)]
    ppermute x8 -> x4, starting transfers between devices: 19.2 us -> 2.94 us  [the longest x2 2.85 us: replica_sum(): x = x + lax.ppermute(x, axis, perm)]
    all_to_all x0 -> x1, starting transfers between devices: none -> 11.3 us  [local(): lax.all_to_all(jnp.broadcast_to(jnp.sum(outer_step * outer_step, axis=(1,...]
    all_to_all x0 -> x1, waiting for transfers between devices: none -> 8.7 us  [local(): lax.all_to_all(jnp.broadcast_to(jnp.sum(outer_step * outer_step, axis=(1,...]
    reduce_sum x1 -> x2, other arithmetic: 1.01 us -> 2.34 us  [the longest x1 2.29 us: local(): jnp.sum(outer_step * outer_step, axis=(1, 2))]
    add x6 -> x3, other arithmetic: 0.16 us -> 1.07 us  [the longest x1 1 us: replica_sum(): x = keep + lax.ppermute(send, axis, swap)]
    unnamed x16 -> x12, local copies, waits for them, and re-layouts: 1.98 us -> 2.73 us
  transfers between devices with their start and end apart: 8 -> 5, of which waited for: 8 -> 5; matrix products, arithmetic and copies ran while one was open for 1% -> 2% of each run, Pallas kernels for 0% -> 0%
where the time goes in v3:
time: 58.9 us; the launch traced here: 58.6 us
  waiting for transfers between devices  24.1 us (41%)
  starting transfers between devices  14.3 us (24%)
  other arithmetic  7.88 us (13%)
  matrix products  6.66 us (11%)
  local copies, waits for them, and re-layouts  4.93 us (8%)
  between operations  0.76 us (1%)
    ppermute x2, waiting for transfers between devices, replica_sum(): x = x + lax.ppermute(x, axis, perm)  12 us
    all_to_all x1, starting transfers between devices, local(): lax.all_to_all(jnp.broadcast_to(jnp.sum(outer_step * outer_step, axis=(1,...  11.3 us
    all_to_all x1, waiting for transfers between devices, local(): lax.all_to_all(jnp.broadcast_to(jnp.sum(outer_step * outer_step, axis=(1,...  8.7 us
    dot_general x1, matrix products, local(): jnp.dot(pseudo_grad.reshape(matrices * rows_dev, model_width), projection...  4.63 us
    convert_element_type x1, other arithmetic, local(): new_params = (anchor_params.astype(jnp.float32) - update.reshape(matrices...  2.87 us
    ppermute x2, starting transfers between devices, replica_sum(): x = x + lax.ppermute(x, axis, perm)  2.85 us
    unnamed x12, local copies, waits for them, and re-layouts  2.73 us
    reduce_sum x1, other arithmetic, local(): jnp.sum(outer_step * outer_step, axis=(1, 2))  2.29 us
  transfers between devices with their start and end apart: 5, of which 5 were waited for; matrix products, arithmetic and copies ran while one was open for 2% of the time, Pallas kernels for 0%

profile of v3, /device:TPU:24, one launch (start us, length us, event | category | flops | bytes accessed | tf_op | source)
XLA Modules:
  0.0 58.6 jit_solution(8915022828740703997)
XLA Ops:
  0.6 0.0 copy-start
  0.7 1.9 %copy-done = bf16[4096,384]{1,0:T(8,128)(2,1)S(1)} copy-done((bf16[4096,384]{1,0:T(8,128)(2,1)S(1)}, bf16[4096,384]{1,0:T(8,128)(2,1)}, u32[]{:S(2)}) %copy-start) | copy-done | bytes 3145752
  2.5 4.6 %fusion.2 = f32[24,16,384]{2,1,0:T(8,128)S(1)} fusion(bf16[24,16,4096]{2,1,0:T(8,128)(2,1)} %param.7, bf16[1,24,16,4096]{3,2,1,0:T(8,128)(2,1)} %param.8, bf16[4096,384]{1,0:T(8,128)(2,1)S(1)} %copy-done), kind=kOutput, calls=%fused_computation.6 | convolution fusion | flops 1214251008 | bytes 10027008 | tf_op jit(solution)/shard_map/dot_general | solution.py:50
  7.2 0.0 copy-start.3
  7.2 0.8 %copy-done.3 = f32[24,16,384]{2,1,0:T(8,128)} copy-done((f32[24,16,384]{2,1,0:T(8,128)}, f32[24,16,384]{2,1,0:T(8,128)S(1)}, u32[]{:S(2)}) %copy-start.3) | copy-done | bytes 589848
  8.0 0.0 copy-start.4
  8.0 0.7 %constant_dynamic-slice_fusion = f32[12,16,384]{2,1,0:T(8,128)} fusion(f32[24,16,384]{2,1,0:T(8,128)S(1)} %fusion.2, s32[]{:T(128)S(6)} %select_n.32), kind=kLoop, calls=%fused_computation.33 | loop fusion | bytes 589828 | tf_op jit(solution)/shard_map/dynamic_slice | solution.py:28
  8.7 0.0 collective-permute-start
  8.7 1.8 %collective-permute-done = f32[12,16,384]{2,1,0:T(8,128)S(1)} collective-permute-done((f32[12,16,384]{2,1,0:T(8,128)}, f32[12,16,384]{2,1,0:T(8,128)S(1)}, u32[]{:S(2)}, u32[]{:S(2)}) %collective-permute-start) | collective-permute-done | bytes 294944 | tf_op jit(solution)/shard_map/ppermute | solution.py:29
  10.5 1.0 %dynamic-slice_add_fusion = f32[12,16,384]{2,1,0:T(8,128)S(1)} fusion(f32[12,16,384]{2,1,0:T(8,128)S(1)} %collective-permute-done, f32[24,16,384]{2,1,0:T(8,128)} %copy-done.3, s32[]{:T(128)S(6)} %select_n.31), kind=kLoop, calls=%fused_computation.20 | loop fusion | flops 73728 | bytes 884740 | tf_op jit(solution)/shard_map/add | solution.py:29
  11.5 0.8 %collective-permute-start.1 = (f32[12,16,384]{2,1,0:T(8,128)S(1)}, f32[12,16,384]{2,1,0:T(8,128)S(1)}, u32[]{:S(2)}, u32[]{:S(2)}) collective-permute-start(f32[12,16,384]{2,1,0:T(8,128)S(1)} %dynamic-slice_add_fusion), channel_id=1, source_target_pairs={{0,64},{64,0},{128,192},{192,128},{96,160},{160,96},{224,32},{32,2... | collective-permute-start | bytes 884744 | tf_op jit(solution)/shard_map/ppermute | solution.py:37
  12.3 6.0 %collective-permute-done.1 = f32[12,16,384]{2,1,0:T(8,128)S(1)} collective-permute-done((f32[12,16,384]{2,1,0:T(8,128)S(1)}, f32[12,16,384]{2,1,0:T(8,128)S(1)}, u32[]{:S(2)}, u32[]{:S(2)}) %collective-permute-start.1) | collective-permute-done | bytes 294944 | tf_op jit(solution)/shard_map/ppermute | solution.py:37
  18.4 2.0 %collective-permute-start.2 = (f32[12,16,384]{2,1,0:T(8,128)S(1)}, f32[12,16,384]{2,1,0:T(8,128)S(1)}, u32[]{:S(2)}, u32[]{:S(2)}) collective-permute-start(f32[12,16,384]{2,1,0:T(8,128)S(1)} %add.40), channel_id=1, source_target_pairs={{64,128},{128,64},{192,0},{0,192},{32,96},{96,32},{160,224},{224,1... | collective-permute-start | bytes 884744 | tf_op jit(solution)/shard_map/ppermute | solution.py:37
  20.4 6.0 %collective-permute-done.2 = f32[12,16,384]{2,1,0:T(8,128)S(1)} collective-permute-done((f32[12,16,384]{2,1,0:T(8,128)S(1)}, f32[12,16,384]{2,1,0:T(8,128)S(1)}, u32[]{:S(2)}, u32[]{:S(2)}) %collective-permute-start.2) | collective-permute-done | bytes 294944 | tf_op jit(solution)/shard_map/ppermute | solution.py:37
  26.4 0.1 collective-permute-start.3
  26.5 0.0 copy-done.4
  26.6 1.7 %collective-permute-done.3 = f32[12,16,384]{2,1,0:T(8,128)} collective-permute-done((f32[12,16,384]{2,1,0:T(8,128)S(1)}, f32[12,16,384]{2,1,0:T(8,128)}, u32[]{:S(2)}, u32[]{:S(2)}) %collective-permute-start.3) | collective-permute-done | bytes 294944 | tf_op jit(solution)/shard_map/ppermute | solution.py:38
  28.2 2.3 %multiply_reduce_fusion = (f32[24]{0:T(128)S(1)}, f32[24,16,384]{2,1,0:T(8,128)}) fusion(f32[12,16,384]{2,1,0:T(8,128)} %collective-permute-done.3, f32[12,16,384]{2,1,0:T(8,128)S(1)} %add.41, pred[]{:T(512)S(6)} %eq.18, f32[24,16,384]{2,1,0:T(8,128)} %param.10), kind=kLoop, calls=%fused_computation.17 | loop fusion | flops 1474536 | bytes 1769569 | tf_op jit(solution)/shard_map/reduce_sum | solution.py:59
  30.5 0.6 %broadcast_in_dim.2 = f32[32,1,24]{2,1,0:T(1,128)} broadcast(f32[24]{0:T(128)S(1)} %get-tuple-element.2), dimensions={2} | broadcast | bytes 3168 | tf_op jit(solution)/shard_map/broadcast_in_dim | solution.py:59
  31.1 11.3 %all-to-all-start = ((f32[32,1,24]{2,1,0:T(1,128)}), f32[32,1,24]{2,1,0:T(1,128)S(1)}, u32[]{:S(2)}, u32[]{:S(2)}) async-start(f32[32,1,24]{2,1,0:T(1,128)} %broadcast_in_dim.2), calls=%async_computation | async-start | bytes 32768 | tf_op jit(solution)/shard_map/all_to_all | solution.py:59
  42.5 0.0 copy-done.5
  42.5 0.2 fusion.12
  42.6 0.0 copy-done.1
  42.6 0.8 %gather_fusion = f32[24]{0:T(128)S(1)} fusion(f32[4,6]{1,0:T(4,128)S(1)} %copy-done.1, s32[24]{0:T(128)S(1)} %fusion.20), kind=kCustom, calls=%fused_computation | custom fusion | bytes 384 | tf_op jit(solution)/shard_map/gather | solution.py:64
  43.5 8.7 %all-to-all-done = f32[32,1,24]{2,1,0:T(1,128)S(1)} async-done(((f32[32,1,24]{2,1,0:T(1,128)}), f32[32,1,24]{2,1,0:T(1,128)S(1)}, u32[]{:S(2)}, u32[]{:S(2)}) %all-to-all-start) | async-done | bytes 3104 | tf_op jit(solution)/shard_map/all_to_all | solution.py:59
  52.2 0.1 reduce_sum.28
  52.2 0.2 fusion.9
  52.4 1.4 %multiply_convert_fusion = bf16[24,16,384]{2,1,0:T(8,128)(2,1)S(1)} fusion(f32[24]{0:T(128)S(1)} %fusion.9, f32[24,16,384]{2,1,0:T(8,128)} %get-tuple-element.3, f32[12,16,384]{2,1,0:T(8,128)} %collective-permute-done.3, f32[12,16,384]{2,1,0:T(8,128)S(1)} %add.41, pred[]{:T(512)S(6)} %eq.18), kind=kLoop, calls=%fused_computation.16 | loop fusion | flops 1179648 | bytes 1474657 | tf_op jit(solution)/shard_map/convert_element_type | solution.py:65
  53.9 0.0 copy-start.2
  53.9 1.8 %convolution_convert_fusion = bf16[384,4096]{1,0:T(8,128)(2,1)S(1)} fusion(bf16[384,384]{1,0:T(8,128)(2,1)S(1)} %bitcast.30, bf16[4096,384]{1,0:T(8,128)(2,1)S(1)} %copy-done), kind=kOutput, calls=%fused_computation.5 | convolution fusion | flops 1209532416 | bytes 6586368 | tf_op jit(solution)/shard_map/dot_general | solution.py:66
  55.7 0.0 copy-done.2
  55.7 2.9 %fusion.1 = bf16[24,16,4096]{2,1,0:T(8,128)(2,1)} fusion(bf16[24,16,4096]{2,1,0:T(8,128)(2,1)S(1)} %copy-done.2, bf16[24,16,4096]{2,1,0:T(8,128)(2,1)S(1)} %bitcast.29), kind=kLoop, calls=%fused_computation.4 | loop fusion | flops 6291456 | bytes 9437184 | tf_op jit(solution)/shard_map/convert_element_type | solution.py:75
  (5 shorter events, 0.1 us)
Async XLA Ops:
  0.6 1.9 %copy-start = (bf16[4096,384]{1,0:T(8,128)(2,1)S(1)}, bf16[4096,384]{1,0:T(8,128)(2,1)}, u32[]{:S(2)}) copy-start(bf16[4096,384]{1,0:T(8,128)(2,1)} %param.9) | copy-start | bytes 9437188
  7.2 0.8 %copy-start.3 = (f32[24,16,384]{2,1,0:T(8,128)}, f32[24,16,384]{2,1,0:T(8,128)S(1)}, u32[]{:S(2)}) copy-start(f32[24,16,384]{2,1,0:T(8,128)S(1)} %fusion.2) | copy-start | bytes 1769476
  8.0 18.6 %copy-start.4 = (s32[24,2]{0,1:T(2,128)S(1)}, s32[24,2]{0,1:T(2,128)}, u32[]{:S(2)}) copy-start(s32[24,2]{0,1:T(2,128)} %param.13) | copy-start | bytes 580
  8.0 34.5 %copy-start.5 = (s32[24]{0:T(128)S(1)}, s32[24]{0:T(128)}, u32[]{:S(2)}) copy-start(s32[24]{0:T(128)} %param.12) | copy-start | bytes 292
  8.0 34.7 %copy-start.1 = (f32[4,6]{1,0:T(4,128)S(1)}, f32[4,6]{1,0:T(4,128)}, u32[]{:S(2)}) copy-start(f32[4,6]{1,0:T(4,128)} %param.11) | copy-start | bytes 292
  8.7 1.8 %collective-permute-start = (f32[12,16,384]{2,1,0:T(8,128)}, f32[12,16,384]{2,1,0:T(8,128)S(1)}, u32[]{:S(2)}, u32[]{:S(2)}) collective-permute-start(f32[12,16,384]{2,1,0:T(8,128)} %constant_dynamic-slice_fusion), channel_id=1, source_target_pairs={{0,32},{32,0},{64,96},{96,64},{128,160},{160,128},{192,224},{224,1... | collective-permute-start | bytes 884744 | tf_op jit(solution)/shard_map/ppermute | solution.py:29
  11.5 6.8 %collective-permute-start.1 = (f32[12,16,384]{2,1,0:T(8,128)S(1)}, f32[12,16,384]{2,1,0:T(8,128)S(1)}, u32[]{:S(2)}, u32[]{:S(2)}) collective-permute-start(f32[12,16,384]{2,1,0:T(8,128)S(1)} %dynamic-slice_add_fusion), channel_id=1, source_target_pairs={{0,64},{64,0},{128,192},{192,128},{96,160},{160,96},{224,32},{32,2... | collective-permute-start | bytes 884744 | tf_op jit(solution)/shard_map/ppermute | solution.py:37
  18.4 8.0 %collective-permute-start.2 = (f32[12,16,384]{2,1,0:T(8,128)S(1)}, f32[12,16,384]{2,1,0:T(8,128)S(1)}, u32[]{:S(2)}, u32[]{:S(2)}) collective-permute-start(f32[12,16,384]{2,1,0:T(8,128)S(1)} %add.40), channel_id=1, source_target_pairs={{64,128},{128,64},{192,0},{0,192},{32,96},{96,32},{160,224},{224,1... | collective-permute-start | bytes 884744 | tf_op jit(solution)/shard_map/ppermute | solution.py:37
  26.4 1.8 %collective-permute-start.3 = (f32[12,16,384]{2,1,0:T(8,128)S(1)}, f32[12,16,384]{2,1,0:T(8,128)}, u32[]{:S(2)}, u32[]{:S(2)}) collective-permute-start(f32[12,16,384]{2,1,0:T(8,128)S(1)} %add.41), channel_id=1, source_target_pairs={{0,32},{32,0},{64,96},{96,64},{128,160},{160,128},{192,224},{224,1... | collective-permute-start | bytes 884744 | tf_op jit(solution)/shard_map/ppermute | solution.py:38
  31.1 21.1 %all-to-all-start = ((f32[32,1,24]{2,1,0:T(1,128)}), f32[32,1,24]{2,1,0:T(1,128)S(1)}, u32[]{:S(2)}, u32[]{:S(2)}) async-start(f32[32,1,24]{2,1,0:T(1,128)} %broadcast_in_dim.2), calls=%async_computation | async-start | bytes 32768 | tf_op jit(solution)/shard_map/all_to_all | solution.py:59
  53.9 1.9 %copy-start.2 = (bf16[24,16,4096]{2,1,0:T(8,128)(2,1)S(1)}, bf16[24,16,4096]{2,1,0:T(8,128)(2,1)}, u32[]{:S(2)}) copy-start(bf16[24,16,4096]{2,1,0:T(8,128)(2,1)} %param.7) | copy-start | bytes 9437188

commit v4 on v1

--- a/solution.py
+++ b/solution.py
@@ -6,25 +6,58 @@
 OUTER_MOMENTUM = 0.9
 EPSILON = 1e-06
 
+def ring_steps(x, axis):
+    even = [(0, 1), (2, 3)]
+    odd = [(1, 2), (3, 0)]
+    for step in range(2):
+        perm = []
+        for c in range(2):
+            for a, b in (even if c == step else odd):
+                perm += [(a * 2 + c, b * 2 + c), (b * 2 + c, a * 2 + c)]
+        x = x + lax.ppermute(x, axis, perm)
+    return x
+
+
+def a2a_sum(v, axis):
+    n = lax.axis_size(axis)
+    return jnp.sum(lax.all_to_all(jnp.broadcast_to(v, (n,) + v.shape), axis, 0, 0, tiled=True), axis=0)
+
 
 def local(anchor_params, replica_params, projection, momentum, rate_table, owner_list, layer_kind):
     matrices, rows_dev, model_width = anchor_params.shape
     rank_dim = projection.shape[1]
     all_rows = rows_dev * lax.axis_size("fsdp")
+    n_replica = lax.axis_size("replica")
     highest = lax.Precision.HIGHEST
-    pseudo_grad = (
-        anchor_params.astype(jnp.float32) - replica_params[0].astype(jnp.float32)
-    ).astype(jnp.bfloat16)
-    compressed = jnp.dot(
-        pseudo_grad.reshape(matrices * rows_dev, model_width),
-        projection,
-        preferred_element_type=jnp.float32,
-    )
-    summed = lax.psum(compressed.reshape(matrices, rows_dev, rank_dim), "replica")
-    outer_grad = summed / lax.axis_size("replica")
+    half = matrices // 2
+    core = lax.axis_index("replica") % 2
+    swap = [(i, i ^ 1) for i in range(n_replica)]
+
+    def compress(first):
+        anchor = lax.dynamic_slice_in_dim(anchor_params, first, half)
+        replica = lax.dynamic_slice_in_dim(replica_params[0], first, half)
+        pseudo_grad = (anchor.astype(jnp.float32) - replica.astype(jnp.float32)).astype(jnp.bfloat16)
+        return jnp.dot(
+            pseudo_grad.reshape(half * rows_dev, model_width), projection, preferred_element_type=jnp.float32
+        ).reshape(half, rows_dev, rank_dim)
+
+    outgoing = lax.ppermute(compress((1 - core) * half), "replica", swap)
+    own = ring_steps(compress(core * half) + outgoing, "replica")
+    own_grad = own / n_replica
+    own_momentum = OUTER_MOMENTUM * lax.dynamic_slice_in_dim(momentum, core * half, half) + own_grad
+    own_step = own_grad + OUTER_MOMENTUM * own_momentum
+    own_squares = a2a_sum(jnp.sum(own_step * own_step, axis=(1, 2)), "fsdp")
+    other = lax.ppermute(own, "replica", swap)
+    summed = jnp.where(core == 1, jnp.concatenate([other, own]), jnp.concatenate([own, other]))
+    outer_grad = summed / n_replica
     new_momentum = OUTER_MOMENTUM * momentum + outer_grad
     outer_step = outer_grad + OUTER_MOMENTUM * new_momentum
-    squares = lax.psum(jnp.sum(outer_step * outer_step, axis=(1, 2)), "fsdp")
+    other_squares = lax.ppermute(own_squares, "replica", swap)
+    squares = jnp.where(
+        core == 1,
+        jnp.concatenate([other_squares, own_squares]),
+        jnp.concatenate([own_squares, other_squares]),
+    )
     same_group = (owner_list[:, None] == owner_list[None, :]).astype(jnp.float32)
     group_squares = jnp.dot(same_group, squares, precision=highest)
     group_count = jnp.sum(same_group, axis=1)

time: 173 us -> 56.8 us (0.33)
  the two profiles are of different devices: /device:TPU:24 before, /device:TPU:1 now
where the time goes in v4:
time: 56.8 us; the launch traced here: 56.6 us
  starting transfers between devices  20.4 us (36%)
  waiting for transfers between devices  18.6 us (33%)
  matrix products  7.85 us (14%)
  other arithmetic  5.6 us (10%)
  local copies, waits for them, and re-layouts  3.39 us (6%)
  between operations  0.73 us (1%)
    ppermute x2, waiting for transfers between devices, ring_steps(): x = x + lax.ppermute(x, axis, perm)  11.6 us
    all_to_all x1, starting transfers between devices, a2a_sum(): lax.all_to_all(jnp.broadcast_to(v, (n,) + v.shape), axis, 0, 0, tiled=True)  9.39 us
    dot_general x2, matrix products, compress(): jnp.dot(pseudo_grad.reshape(half * rows_dev, model_width), projection, pr...  5.82 us
    all_to_all x1, waiting for transfers between devices, a2a_sum(): lax.all_to_all(jnp.broadcast_to(v, (n,) + v.shape), axis, 0, 0, tiled=True)  4.88 us
    ppermute x1, starting transfers between devices, local(): other_squares = lax.ppermute(own_squares, 'replica', swap)  3.82 us
    ppermute x1, starting transfers between devices, local(): outgoing = lax.ppermute(compress((1 - core) * half), 'replica', swap)  3.29 us
    convert_element_type x1, other arithmetic, local(): new_params = (anchor_params.astype(jnp.float32) - update.reshape(matrices...  2.87 us
    ppermute x1, starting transfers between devices, local(): other = lax.ppermute(own, 'replica', swap)  2.68 us
  transfers between devices with their start and end apart: 6, of which 5 were waited for; matrix products, arithmetic and copies ran while one was open for 2% of the time, Pallas kernels for 0%

profile of v4, /device:TPU:1, one launch (start us, length us, event | category | flops | bytes accessed | tf_op | source)
XLA Modules:
  0.0 56.6 jit_solution(6540779964678806313)
XLA Ops:
  0.6 0.0 copy-start
  0.7 1.9 %copy-done = bf16[4096,384]{1,0:T(8,128)(2,1)S(1)} copy-done((bf16[4096,384]{1,0:T(8,128)(2,1)S(1)}, bf16[4096,384]{1,0:T(8,128)(2,1)}, u32[]{:S(2)}) %copy-start) | copy-done | bytes 3145752
  2.5 2.9 %fusion.3 = f32[12,16,384]{2,1,0:T(8,128)S(1)} fusion(bf16[4096,384]{1,0:T(8,128)(2,1)S(1)} %copy-done, bf16[1,24,16,4096]{3,2,1,0:T(8,128)(2,1)} %param.8, s32[]{:T(128)S(6)} %select_n.43, bf16[24,16,4096]{2,1,0:T(8,128)(2,1)} %param.7), kind=kOutput, calls=%fused_computation.8 | convolution fusion | flops 607125504 | bytes 6586372 | tf_op jit(solution)/shard_map/dot_general | solution.py:40
  5.4 3.3 %collective-permute-start = (f32[12,16,384]{2,1,0:T(8,128)S(1)}, f32[12,16,384]{2,1,0:T(8,128)}, u32[]{:S(2)}, u32[]{:S(2)}) collective-permute-start(f32[12,16,384]{2,1,0:T(8,128)S(1)} %fusion.3), channel_id=1, source_target_pairs={{0,32},{32,0},{64,96},{96,64},{128,160},{160,128},{192,224},{224,1... | collective-permute-start | bytes 884744 | tf_op jit(solution)/shard_map/ppermute | solution.py:44
  8.7 0.0 copy-start.4
  8.7 0.0 copy-start.3
  8.7 1.3 %collective-permute-done = f32[12,16,384]{2,1,0:T(8,128)} collective-permute-done((f32[12,16,384]{2,1,0:T(8,128)S(1)}, f32[12,16,384]{2,1,0:T(8,128)}, u32[]{:S(2)}, u32[]{:S(2)}) %collective-permute-start) | collective-permute-done | bytes 294944 | tf_op jit(solution)/shard_map/ppermute | solution.py:44
  10.1 2.9 %fusion.15 = f32[12,16,384]{2,1,0:T(8,128)S(1)} fusion(f32[12,16,384]{2,1,0:T(8,128)} %collective-permute-done, bf16[4096,384]{1,0:T(8,128)(2,1)S(1)} %copy-done, bf16[1,24,16,4096]{3,2,1,0:T(8,128)(2,1)} %param.8, s32[]{:T(128)S(6)} %select_n.42, bf16[24,16,4096]{2,1,0:T(8,128)(2,1)} %param.7), kind=kOutput, calls=%fused_computation.18 | convolution fusion | flops 607199232 | bytes 6881284 | tf_op jit(solution)/shard_map/dot_general | solution.py:40
  13.0 1.1 %collective-permute-start.1 = (f32[12,16,384]{2,1,0:T(8,128)S(1)}, f32[12,16,384]{2,1,0:T(8,128)S(1)}, u32[]{:S(2)}, u32[]{:S(2)}) collective-permute-start(f32[12,16,384]{2,1,0:T(8,128)S(1)} %fusion.15), channel_id=1, source_target_pairs={{0,64},{64,0},{128,192},{192,128},{96,160},{160,96},{224,32},{32,2... | collective-permute-start | bytes 884744 | tf_op jit(solution)/shard_map/ppermute | solution.py:17
  14.1 5.8 %collective-permute-done.1 = f32[12,16,384]{2,1,0:T(8,128)S(1)} collective-permute-done((f32[12,16,384]{2,1,0:T(8,128)S(1)}, f32[12,16,384]{2,1,0:T(8,128)S(1)}, u32[]{:S(2)}, u32[]{:S(2)}) %collective-permute-start.1) | collective-permute-done | bytes 294944 | tf_op jit(solution)/shard_map/ppermute | solution.py:17
  19.9 0.1 collective-permute-start.2
  20.0 0.0 copy-done.4
  20.0 5.8 %collective-permute-done.2 = f32[12,16,384]{2,1,0:T(8,128)S(1)} collective-permute-done((f32[12,16,384]{2,1,0:T(8,128)S(1)}, f32[12,16,384]{2,1,0:T(8,128)S(1)}, u32[]{:S(2)}, u32[]{:S(2)}) %collective-permute-start.2) | collective-permute-done | bytes 294944 | tf_op jit(solution)/shard_map/ppermute | solution.py:17
  25.9 0.0 copy-done.3
  25.9 0.2 multiply_reduce_fusion
  26.1 0.6 %broadcast_in_dim.2 = f32[32,1,12]{2,1,0:T(1,128)} broadcast(f32[12]{0:T(128)S(1)} %get-tuple-element.4), dimensions={2} | broadcast | bytes 1584 | tf_op jit(solution)/shard_map/broadcast_in_dim | solution.py:23
  26.7 9.4 %all-to-all-start = ((f32[32,1,12]{2,1,0:T(1,128)}), f32[32,1,12]{2,1,0:T(1,128)S(1)}, u32[]{:S(2)}, u32[]{:S(2)}) async-start(f32[32,1,12]{2,1,0:T(1,128)} %broadcast_in_dim.2), calls=%async_computation | async-start | bytes 32768 | tf_op jit(solution)/shard_map/all_to_all | solution.py:23
  36.1 2.7 %collective-permute-start.3 = (f32[12,16,384]{2,1,0:T(8,128)S(1)}, f32[12,16,384]{2,1,0:T(8,128)}, u32[]{:S(2)}, u32[]{:S(2)}) collective-permute-start(f32[12,16,384]{2,1,0:T(8,128)S(1)} %get-tuple-element.5), channel_id=1, source_target_pairs={{0,32},{32,0},{64,96},{96,64},{128,160},{160,128},{192,224},{224,1... | collective-permute-start | bytes 884744 | tf_op jit(solution)/shard_map/ppermute | solution.py:50
  38.8 0.0 copy-done.5
  38.8 0.2 fusion.26
  38.9 0.0 copy-done.1
  38.9 0.8 %gather_fusion = f32[24]{0:T(128)S(1)} fusion(f32[4,6]{1,0:T(4,128)S(1)} %copy-done.1, s32[24]{0:T(128)S(1)} %fusion.44), kind=kCustom, calls=%fused_computation | custom fusion | bytes 384 | tf_op jit(solution)/shard_map/gather | solution.py:65
  39.8 4.9 %all-to-all-done = f32[32,1,12]{2,1,0:T(1,128)S(1)} async-done(((f32[32,1,12]{2,1,0:T(1,128)}), f32[32,1,12]{2,1,0:T(1,128)S(1)}, u32[]{:S(2)}, u32[]{:S(2)}) %all-to-all-start) | async-done | bytes 1568 | tf_op jit(solution)/shard_map/all_to_all | solution.py:23
  44.7 0.1 reduce_sum.28
  44.7 3.8 %collective-permute-start.4 = (f32[12]{0:T(128)S(1)}, f32[12]{0:T(128)S(1)}, u32[]{:S(2)}, u32[]{:S(2)}) collective-permute-start(f32[12]{0:T(128)S(1)} %reduce_sum.28), channel_id=1, source_target_pairs={{0,32},{32,0},{64,96},{96,64},{128,160},{160,128},{192,224},{224,1... | collective-permute-start | bytes 152 | tf_op jit(solution)/shard_map/ppermute | solution.py:55
  48.5 0.8 %collective-permute-done.4 = f32[12]{0:T(128)S(1)} collective-permute-done((f32[12]{0:T(128)S(1)}, f32[12]{0:T(128)S(1)}, u32[]{:S(2)}, u32[]{:S(2)}) %collective-permute-start.4) | collective-permute-done | bytes 80 | tf_op jit(solution)/shard_map/ppermute | solution.py:55
  49.4 0.2 fusion.23
  49.6 0.0 collective-permute-done.3
  49.6 2.3 %multiply_convert_fusion = (bf16[24,16,384]{2,1,0:T(8,128)(2,1)S(1)}, f32[24,16,384]{2,1,0:T(8,128)}) fusion(f32[12,16,384]{2,1,0:T(8,128)} %collective-permute-done.3, f32[12,16,384]{2,1,0:T(8,128)S(1)} %get-tuple-element.5, f32[24]{0:T(128)S(1)} %fusion.23, pred[]{:T(512)S(6)} %eq.10, f32[24,16,384]{2,1,0:T(8,128)} %param.10), kind=kLoop, calls=%fused_computation.26 | loop fusion | flops 1474560 | bytes 2064481 | tf_op jit(solution)/shard_map/convert_element_type | solution.py:66
  51.8 1.8 %convolution_convert_fusion = bf16[384,4096]{1,0:T(8,128)(2,1)S(1)} fusion(bf16[384,384]{1,0:T(8,128)(2,1)S(1)} %bitcast.42, bf16[4096,384]{1,0:T(8,128)(2,1)S(1)} %copy-done), kind=kOutput, calls=%fused_computation.3 | convolution fusion | flops 1209532416 | bytes 6586368 | tf_op jit(solution)/shard_map/dot_general | solution.py:67
  53.7 0.0 copy-done.2
  53.7 2.9 %fusion = bf16[24,16,4096]{2,1,0:T(8,128)(2,1)} fusion(bf16[24,16,4096]{2,1,0:T(8,128)(2,1)S(1)} %bitcast.41, bf16[24,16,4096]{2,1,0:T(8,128)(2,1)S(1)} %copy-done.2), kind=kLoop, calls=%fused_computation.2 | loop fusion | flops 6291456 | bytes 9437184 | tf_op jit(solution)/shard_map/convert_element_type | solution.py:76
  (5 shorter events, 0.0 us)
Async XLA Ops:
  0.6 1.9 %copy-start = (bf16[4096,384]{1,0:T(8,128)(2,1)S(1)}, bf16[4096,384]{1,0:T(8,128)(2,1)}, u32[]{:S(2)}) copy-start(bf16[4096,384]{1,0:T(8,128)(2,1)} %param.9) | copy-start | bytes 9437188
  5.4 4.6 %collective-permute-start = (f32[12,16,384]{2,1,0:T(8,128)S(1)}, f32[12,16,384]{2,1,0:T(8,128)}, u32[]{:S(2)}, u32[]{:S(2)}) collective-permute-start(f32[12,16,384]{2,1,0:T(8,128)S(1)} %fusion.3), channel_id=1, source_target_pairs={{0,32},{32,0},{64,96},{96,64},{128,160},{160,128},{192,224},{224,1... | collective-permute-start | bytes 884744 | tf_op jit(solution)/shard_map/ppermute | solution.py:44
  8.7 11.3 %copy-start.4 = (s32[24,2]{0,1:T(2,128)S(1)}, s32[24,2]{0,1:T(2,128)}, u32[]{:S(2)}) copy-start(s32[24,2]{0,1:T(2,128)} %param.13) | copy-start | bytes 580
  8.7 17.1 %copy-start.3 = (f32[24,16,384]{2,1,0:T(8,128)S(1)}, f32[24,16,384]{2,1,0:T(8,128)}, u32[]{:S(2)}) copy-start(f32[24,16,384]{2,1,0:T(8,128)} %param.10) | copy-start | bytes 1769476
  8.7 30.0 %copy-start.5 = (s32[24]{0:T(128)S(1)}, s32[24]{0:T(128)}, u32[]{:S(2)}) copy-start(s32[24]{0:T(128)} %param.12) | copy-start | bytes 292
  8.7 30.2 %copy-start.1 = (f32[4,6]{1,0:T(4,128)S(1)}, f32[4,6]{1,0:T(4,128)}, u32[]{:S(2)}) copy-start(f32[4,6]{1,0:T(4,128)} %param.11) | copy-start | bytes 292
  13.0 6.9 %collective-permute-start.1 = (f32[12,16,384]{2,1,0:T(8,128)S(1)}, f32[12,16,384]{2,1,0:T(8,128)S(1)}, u32[]{:S(2)}, u32[]{:S(2)}) collective-permute-start(f32[12,16,384]{2,1,0:T(8,128)S(1)} %fusion.15), channel_id=1, source_target_pairs={{0,64},{64,0},{128,192},{192,128},{96,160},{160,96},{224,32},{32,2... | collective-permute-start | bytes 884744 | tf_op jit(solution)/shard_map/ppermute | solution.py:17
  19.9 6.0 %collective-permute-start.2 = (f32[12,16,384]{2,1,0:T(8,128)S(1)}, f32[12,16,384]{2,1,0:T(8,128)S(1)}, u32[]{:S(2)}, u32[]{:S(2)}) collective-permute-start(f32[12,16,384]{2,1,0:T(8,128)S(1)} %add.49), channel_id=1, source_target_pairs={{64,128},{128,64},{192,0},{0,192},{32,96},{96,32},{160,224},{224,1... | collective-permute-start | bytes 884744 | tf_op jit(solution)/shard_map/ppermute | solution.py:17
  26.7 18.0 %all-to-all-start = ((f32[32,1,12]{2,1,0:T(1,128)}), f32[32,1,12]{2,1,0:T(1,128)S(1)}, u32[]{:S(2)}, u32[]{:S(2)}) async-start(f32[32,1,12]{2,1,0:T(1,128)} %broadcast_in_dim.2), calls=%async_computation | async-start | bytes 32768 | tf_op jit(solution)/shard_map/all_to_all | solution.py:23
  36.1 13.5 %collective-permute-start.3 = (f32[12,16,384]{2,1,0:T(8,128)S(1)}, f32[12,16,384]{2,1,0:T(8,128)}, u32[]{:S(2)}, u32[]{:S(2)}) collective-permute-start(f32[12,16,384]{2,1,0:T(8,128)S(1)} %get-tuple-element.5), channel_id=1, source_target_pairs={{0,32},{32,0},{64,96},{96,64},{128,160},{160,128},{192,224},{224,1... | collective-permute-start | bytes 884744 | tf_op jit(solution)/shard_map/ppermute | solution.py:50
  44.7 4.6 %collective-permute-start.4 = (f32[12]{0:T(128)S(1)}, f32[12]{0:T(128)S(1)}, u32[]{:S(2)}, u32[]{:S(2)}) collective-permute-start(f32[12]{0:T(128)S(1)} %reduce_sum.28), channel_id=1, source_target_pairs={{0,32},{32,0},{64,96},{96,64},{128,160},{160,128},{192,224},{224,1... | collective-permute-start | bytes 152 | tf_op jit(solution)/shard_map/ppermute | solution.py:55
  51.8 1.9 %copy-start.2 = (bf16[24,16,4096]{2,1,0:T(8,128)(2,1)S(1)}, bf16[24,16,4096]{2,1,0:T(8,128)(2,1)}, u32[]{:S(2)}) copy-start(bf16[24,16,4096]{2,1,0:T(8,128)(2,1)} %param.7) | copy-start | bytes 9437188

commit v5 on v4

--- a/solution.py
+++ b/solution.py
@@ -42,7 +42,7 @@
         ).reshape(half, rows_dev, rank_dim)
 
     outgoing = lax.ppermute(compress((1 - core) * half), "replica", swap)
-    own = ring_steps(compress(core * half) + outgoing, "replica")
+    own = ring_steps(lax.optimization_barrier(compress(core * half)) + outgoing, "replica")
     own_grad = own / n_replica
     own_momentum = OUTER_MOMENTUM * lax.dynamic_slice_in_dim(momentum, core * half, half) + own_grad
     own_step = own_grad + OUTER_MOMENTUM * own_momentum

time: 56.8 us -> 55.8 us (0.982)
  waiting for transfers between devices: 18.6 us -> 17.6 us
  starting transfers between devices: 20.4 us -> 19.6 us
  matrix products: 7.85 us -> 8.57 us
    ppermute x1, waiting for transfers between devices: 1.33 us -> 0.01 us  [local(): outgoing = lax.ppermute(compress((1 - core) * half), 'replica', swap)]
    dot_general x2, matrix products: 5.82 us -> 6.54 us  [compress(): jnp.dot(pseudo_grad.reshape(half * rows_dev, model_width), projection, pr...]
  transfers between devices with their start and end apart: 6 -> 6, of which waited for: 5 -> 4; matrix products, arithmetic and copies ran while one was open for 2% -> 8% of each run, Pallas kernels for 0% -> 0%
where the time goes in v5:
time: 55.8 us; the launch traced here: 55.6 us
  starting transfers between devices  19.6 us (35%)
  waiting for transfers between devices  17.6 us (32%)
  matrix products  8.57 us (15%)
  other arithmetic  5.63 us (10%)
  local copies, waits for them, and re-layouts  3.4 us (6%)
  between operations  0.75 us (1%)
    ppermute x2, waiting for transfers between devices, ring_steps(): x = x + lax.ppermute(x, axis, perm)  11.6 us
    all_to_all x1, starting transfers between devices, a2a_sum(): lax.all_to_all(jnp.broadcast_to(v, (n,) + v.shape), axis, 0, 0, tiled=True)  9.4 us
    dot_general x2, matrix products, compress(): jnp.dot(pseudo_grad.reshape(half * rows_dev, model_width), projection, pr...  6.54 us
    all_to_all x1, waiting for transfers between devices, a2a_sum(): lax.all_to_all(jnp.broadcast_to(v, (n,) + v.shape), axis, 0, 0, tiled=True)  5.22 us
    ppermute x1, starting transfers between devices, local(): other_squares = lax.ppermute(own_squares, 'replica', swap)  3.47 us
    ppermute x1, starting transfers between devices, local(): outgoing = lax.ppermute(compress((1 - core) * half), 'replica', swap)  3.2 us
    convert_element_type x1, other arithmetic, local(): new_params = (anchor_params.astype(jnp.float32) - update.reshape(matrices...  2.87 us
    ppermute x1, starting transfers between devices, local(): other = lax.ppermute(own, 'replica', swap)  2.33 us
  transfers between devices with their start and end apart: 6, of which 4 were waited for; matrix products, arithmetic and copies ran while one was open for 8% of the time, Pallas kernels for 0%

profile of v5, /device:TPU:1, one launch (start us, length us, event | category | flops | bytes accessed | tf_op | source)
XLA Modules:
  0.0 55.6 jit_solution(2674979834244888041)
XLA Ops:
  0.6 0.0 copy-start
  0.7 1.9 %copy-done = bf16[4096,384]{1,0:T(8,128)(2,1)S(1)} copy-done((bf16[4096,384]{1,0:T(8,128)(2,1)S(1)}, bf16[4096,384]{1,0:T(8,128)(2,1)}, u32[]{:S(2)}) %copy-start) | copy-done | bytes 3145752
  2.5 3.6 %fusion.3 = f32[12,16,384]{2,1,0:T(8,128)} fusion(bf16[4096,384]{1,0:T(8,128)(2,1)S(1)} %copy-done, bf16[1,24,16,4096]{3,2,1,0:T(8,128)(2,1)} %param.8, s32[]{:T(128)S(6)} %select_n.43, bf16[24,16,4096]{2,1,0:T(8,128)(2,1)} %param.7), kind=kOutput, calls=%fused_computation.8 | convolution fusion | flops 607125504 | bytes 6586372 | tf_op jit(solution)/shard_map/dot_general | solution.py:40
  6.1 3.2 %collective-permute-start = (f32[12,16,384]{2,1,0:T(8,128)}, f32[12,16,384]{2,1,0:T(8,128)S(1)}, u32[]{:S(2)}, u32[]{:S(2)}) collective-permute-start(f32[12,16,384]{2,1,0:T(8,128)} %fusion.3), channel_id=1, source_target_pairs={{0,32},{32,0},{64,96},{96,64},{128,160},{160,128},{192,224},{224,1... | collective-permute-start | bytes 884744 | tf_op jit(solution)/shard_map/ppermute | solution.py:44
  9.3 0.0 copy-start.3
  9.3 3.0 %fusion.5 = f32[12,16,384]{2,1,0:T(8,128)S(1)} fusion(bf16[4096,384]{1,0:T(8,128)(2,1)S(1)} %copy-done, bf16[1,24,16,4096]{3,2,1,0:T(8,128)(2,1)} %param.8, s32[]{:T(128)S(6)} %select_n.42, bf16[24,16,4096]{2,1,0:T(8,128)(2,1)} %param.7), kind=kOutput, calls=%fused_computation.10 | convolution fusion | flops 607125504 | bytes 6586372 | tf_op jit(solution)/shard_map/dot_general | solution.py:40
  12.3 0.0 copy-start.1
  12.3 0.0 collective-permute-done
  12.3 1.1 %collective-permute-start.1 = (f32[12,16,384]{2,1,0:T(8,128)S(1)}, f32[12,16,384]{2,1,0:T(8,128)S(1)}, u32[]{:S(2)}, u32[]{:S(2)}) collective-permute-start(f32[12,16,384]{2,1,0:T(8,128)S(1)} %add.48), channel_id=1, source_target_pairs={{0,64},{64,0},{128,192},{192,128},{96,160},{160,96},{224,32},{32,2... | collective-permute-start | bytes 884744 | tf_op jit(solution)/shard_map/ppermute | solution.py:17
  13.5 5.8 %collective-permute-done.1 = f32[12,16,384]{2,1,0:T(8,128)S(1)} collective-permute-done((f32[12,16,384]{2,1,0:T(8,128)S(1)}, f32[12,16,384]{2,1,0:T(8,128)S(1)}, u32[]{:S(2)}, u32[]{:S(2)}) %collective-permute-start.1) | collective-permute-done | bytes 294944 | tf_op jit(solution)/shard_map/ppermute | solution.py:17
  19.3 0.1 collective-permute-start.2
  19.4 0.0 copy-done.4
  19.4 5.8 %collective-permute-done.2 = f32[12,16,384]{2,1,0:T(8,128)S(1)} collective-permute-done((f32[12,16,384]{2,1,0:T(8,128)S(1)}, f32[12,16,384]{2,1,0:T(8,128)S(1)}, u32[]{:S(2)}, u32[]{:S(2)}) %collective-permute-start.2) | collective-permute-done | bytes 294944 | tf_op jit(solution)/shard_map/ppermute | solution.py:17
  25.2 0.0 copy-done.3
  25.2 0.2 multiply_reduce_fusion
  25.4 0.6 %broadcast_in_dim.2 = f32[32,1,12]{2,1,0:T(1,128)} broadcast(f32[12]{0:T(128)S(1)} %get-tuple-element.4), dimensions={2} | broadcast | bytes 1584 | tf_op jit(solution)/shard_map/broadcast_in_dim | solution.py:23
  26.0 9.4 %all-to-all-start = ((f32[32,1,12]{2,1,0:T(1,128)}), f32[32,1,12]{2,1,0:T(1,128)S(1)}, u32[]{:S(2)}, u32[]{:S(2)}) async-start(f32[32,1,12]{2,1,0:T(1,128)} %broadcast_in_dim.2), calls=%async_computation | async-start | bytes 32768 | tf_op jit(solution)/shard_map/all_to_all | solution.py:23
  35.4 2.3 %collective-permute-start.3 = (f32[12,16,384]{2,1,0:T(8,128)S(1)}, f32[12,16,384]{2,1,0:T(8,128)}, u32[]{:S(2)}, u32[]{:S(2)}) collective-permute-start(f32[12,16,384]{2,1,0:T(8,128)S(1)} %get-tuple-element.5), channel_id=1, source_target_pairs={{0,32},{32,0},{64,96},{96,64},{128,160},{160,128},{192,224},{224,1... | collective-permute-start | bytes 884744 | tf_op jit(solution)/shard_map/ppermute | solution.py:50
  37.8 0.0 copy-done.5
  37.8 0.2 fusion.21
  37.9 0.0 copy-done.1
  38.0 0.8 %gather_fusion = f32[24]{0:T(128)S(1)} fusion(f32[4,6]{1,0:T(4,128)S(1)} %copy-done.1, s32[24]{0:T(128)S(1)} %fusion.39), kind=kCustom, calls=%fused_computation | custom fusion | bytes 384 | tf_op jit(solution)/shard_map/gather | solution.py:65
  38.8 5.2 %all-to-all-done = f32[32,1,12]{2,1,0:T(1,128)S(1)} async-done(((f32[32,1,12]{2,1,0:T(1,128)}), f32[32,1,12]{2,1,0:T(1,128)S(1)}, u32[]{:S(2)}, u32[]{:S(2)}) %all-to-all-start) | async-done | bytes 1568 | tf_op jit(solution)/shard_map/all_to_all | solution.py:23
  44.0 0.1 reduce_sum.28
  44.1 3.5 %collective-permute-start.4 = (f32[12]{0:T(128)S(1)}, f32[12]{0:T(128)S(1)}, u32[]{:S(2)}, u32[]{:S(2)}) collective-permute-start(f32[12]{0:T(128)S(1)} %reduce_sum.28), channel_id=1, source_target_pairs={{0,32},{32,0},{64,96},{96,64},{128,160},{160,128},{192,224},{224,1... | collective-permute-start | bytes 152 | tf_op jit(solution)/shard_map/ppermute | solution.py:55
  47.5 0.8 %collective-permute-done.4 = f32[12]{0:T(128)S(1)} collective-permute-done((f32[12]{0:T(128)S(1)}, f32[12]{0:T(128)S(1)}, u32[]{:S(2)}, u32[]{:S(2)}) %collective-permute-start.4) | collective-permute-done | bytes 80 | tf_op jit(solution)/shard_map/ppermute | solution.py:55
  48.4 0.2 fusion.18
  48.6 0.0 collective-permute-done.3
  48.6 2.3 %multiply_convert_fusion = (bf16[24,16,384]{2,1,0:T(8,128)(2,1)S(1)}, f32[24,16,384]{2,1,0:T(8,128)}) fusion(f32[12,16,384]{2,1,0:T(8,128)} %collective-permute-done.3, f32[12,16,384]{2,1,0:T(8,128)S(1)} %get-tuple-element.5, f32[24]{0:T(128)S(1)} %fusion.18, pred[]{:T(512)S(6)} %eq.10, f32[24,16,384]{2,1,0:T(8,128)} %param.10), kind=kLoop, calls=%fused_computation.25 | loop fusion | flops 1474560 | bytes 2064481 | tf_op jit(solution)/shard_map/convert_element_type | solution.py:66
  50.8 1.8 %convolution_convert_fusion = bf16[384,4096]{1,0:T(8,128)(2,1)S(1)} fusion(bf16[384,384]{1,0:T(8,128)(2,1)S(1)} %bitcast.38, bf16[4096,384]{1,0:T(8,128)(2,1)S(1)} %copy-done), kind=kOutput, calls=%fused_computation.3 | convolution fusion | flops 1209532416 | bytes 6586368 | tf_op jit(solution)/shard_map/dot_general | solution.py:67
  52.7 0.0 copy-done.2
  52.7 2.9 %fusion = bf16[24,16,4096]{2,1,0:T(8,128)(2,1)} fusion(bf16[24,16,4096]{2,1,0:T(8,128)(2,1)S(1)} %bitcast.37, bf16[24,16,4096]{2,1,0:T(8,128)(2,1)S(1)} %copy-done.2), kind=kLoop, calls=%fused_computation.2 | loop fusion | flops 6291456 | bytes 9437184 | tf_op jit(solution)/shard_map/convert_element_type | solution.py:76
  (6 shorter events, 0.1 us)
Async XLA Ops:
  0.6 1.9 %copy-start = (bf16[4096,384]{1,0:T(8,128)(2,1)S(1)}, bf16[4096,384]{1,0:T(8,128)(2,1)}, u32[]{:S(2)}) copy-start(bf16[4096,384]{1,0:T(8,128)(2,1)} %param.9) | copy-start | bytes 9437188
  6.1 6.2 %collective-permute-start = (f32[12,16,384]{2,1,0:T(8,128)}, f32[12,16,384]{2,1,0:T(8,128)S(1)}, u32[]{:S(2)}, u32[]{:S(2)}) collective-permute-start(f32[12,16,384]{2,1,0:T(8,128)} %fusion.3), channel_id=1, source_target_pairs={{0,32},{32,0},{64,96},{96,64},{128,160},{160,128},{192,224},{224,1... | collective-permute-start | bytes 884744 | tf_op jit(solution)/shard_map/ppermute | solution.py:44
  9.3 10.0 %copy-start.4 = (s32[24,2]{0,1:T(2,128)S(1)}, s32[24,2]{0,1:T(2,128)}, u32[]{:S(2)}) copy-start(s32[24,2]{0,1:T(2,128)} %param.13) | copy-start | bytes 580
  9.3 15.9 %copy-start.3 = (f32[24,16,384]{2,1,0:T(8,128)S(1)}, f32[24,16,384]{2,1,0:T(8,128)}, u32[]{:S(2)}) copy-start(f32[24,16,384]{2,1,0:T(8,128)} %param.10) | copy-start | bytes 1769476
  9.3 28.5 %copy-start.5 = (s32[24]{0:T(128)S(1)}, s32[24]{0:T(128)}, u32[]{:S(2)}) copy-start(s32[24]{0:T(128)} %param.12) | copy-start | bytes 292
  12.3 25.7 %copy-start.1 = (f32[4,6]{1,0:T(4,128)S(1)}, f32[4,6]{1,0:T(4,128)}, u32[]{:S(2)}) copy-start(f32[4,6]{1,0:T(4,128)} %param.11) | copy-start | bytes 292
  12.3 6.9 %collective-permute-start.1 = (f32[12,16,384]{2,1,0:T(8,128)S(1)}, f32[12,16,384]{2,1,0:T(8,128)S(1)}, u32[]{:S(2)}, u32[]{:S(2)}) collective-permute-start(f32[12,16,384]{2,1,0:T(8,128)S(1)} %add.48), channel_id=1, source_target_pairs={{0,64},{64,0},{128,192},{192,128},{96,160},{160,96},{224,32},{32,2... | collective-permute-start | bytes 884744 | tf_op jit(solution)/shard_map/ppermute | solution.py:17
  19.3 6.0 %collective-permute-start.2 = (f32[12,16,384]{2,1,0:T(8,128)S(1)}, f32[12,16,384]{2,1,0:T(8,128)S(1)}, u32[]{:S(2)}, u32[]{:S(2)}) collective-permute-start(f32[12,16,384]{2,1,0:T(8,128)S(1)} %add.49), channel_id=1, source_target_pairs={{64,128},{128,64},{192,0},{0,192},{32,96},{96,32},{160,224},{224,1... | collective-permute-start | bytes 884744 | tf_op jit(solution)/shard_map/ppermute | solution.py:17
  26.0 18.0 %all-to-all-start = ((f32[32,1,12]{2,1,0:T(1,128)}), f32[32,1,12]{2,1,0:T(1,128)S(1)}, u32[]{:S(2)}, u32[]{:S(2)}) async-start(f32[32,1,12]{2,1,0:T(1,128)} %broadcast_in_dim.2), calls=%async_computation | async-start | bytes 32768 | tf_op jit(solution)/shard_map/all_to_all | solution.py:23
  35.4 13.1 %collective-permute-start.3 = (f32[12,16,384]{2,1,0:T(8,128)S(1)}, f32[12,16,384]{2,1,0:T(8,128)}, u32[]{:S(2)}, u32[]{:S(2)}) collective-permute-start(f32[12,16,384]{2,1,0:T(8,128)S(1)} %get-tuple-element.5), channel_id=1, source_target_pairs={{0,32},{32,0},{64,96},{96,64},{128,160},{160,128},{192,224},{224,1... | collective-permute-start | bytes 884744 | tf_op jit(solution)/shard_map/ppermute | solution.py:50
  44.1 4.3 %collective-permute-start.4 = (f32[12]{0:T(128)S(1)}, f32[12]{0:T(128)S(1)}, u32[]{:S(2)}, u32[]{:S(2)}) collective-permute-start(f32[12]{0:T(128)S(1)} %reduce_sum.28), channel_id=1, source_target_pairs={{0,32},{32,0},{64,96},{96,64},{128,160},{160,128},{192,224},{224,1... | collective-permute-start | bytes 152 | tf_op jit(solution)/shard_map/ppermute | solution.py:55
  50.8 1.9 %copy-start.2 = (bf16[24,16,4096]{2,1,0:T(8,128)(2,1)S(1)}, bf16[24,16,4096]{2,1,0:T(8,128)(2,1)}, u32[]{:S(2)}) copy-start(bf16[24,16,4096]{2,1,0:T(8,128)(2,1)} %param.7) | copy-start | bytes 9437188
